TPU v7x, 256 devices: a whole 4x4x8 slice. The times are simulated.
256 devices in a mesh: ctx: 64 (over x_hi, z, y), mp: 4 (over x_lo, core).
Axes of the slice: x: 4 (x_hi: 2, x_lo: 2; x = x_hi * 2 + x_lo), y: 4, z: 8, core: 2. Of those that a mesh axis runs over, the one named last changes fastest.
Arguments:
- q_mr: bfloat16 [16384, 4096], P('ctx', 'mp'), may hold values from -6 to 6
- k_mr: bfloat16 [16384, 4096], P('ctx', 'mp'), may hold values from -6 to 6
- v_mr: bfloat16 [16384, 4096], P('ctx', 'mp'), may hold values from -6 to 6
- q_li: bfloat16 [16384, 4096], P('ctx', 'mp'), may hold values from -6 to 6
- k_li: bfloat16 [16384, 4096], P('ctx', 'mp'), may hold values from -6 to 6
- short_taps: float32 [6, 3, 4096], P(None, None, 'mp'), may hold values from -3.5 to 3.5
- mr_taps: float32 [128, 4096], P(None, 'mp'), may hold values from -0.5 to 0.5
- norm_gain: float32 [4096], P('mp'), may hold values from 0.1 to 1.9
- decay_rate: float32 [16, 4096], P(None, 'mp'), may hold values from 1.8310548e-05 to 0.03
- residue: float32 [16, 4096], P(None, 'mp'), may hold values from -1.5 to 1.5
Outputs:
- mixer_mr: bfloat16 [16384, 4096], P('ctx', 'mp')
- mixer_li: bfloat16 [16384, 4096], P('ctx', 'mp')
All inputs are finite; a program needn't handle non-finite values.
Results may differ from a plain program's by a relative error of at most 0.0078.
Values may be sent and summed in bfloat16 or wider, within the bound.
No kernel may reach another device: no remote copies, remote signals or barrier semaphores. Data moves between devices by JAX's collectives and lax.ppermute only.
A program may use at most 64 MiB of HBM per device.

v0:
```python
import jax
import jax.numpy as jnp
from jax import lax
from jax.sharding import PartitionSpec as P

D = 4096


def shifted(shard, axis, by):
    devices = lax.axis_size(axis)
    pairs = [(i, i + by) for i in range(devices) if 0 <= i + by < devices]
    return lax.ppermute(shard, axis, pairs)


def settle(values):
    return lax.optimization_barrier(values.astype(jnp.bfloat16))


def causal_conv(extended, taps):
    kernel = taps[::-1][:, None, :]
    return lax.conv_general_dilated(
        extended,
        kernel,
        (1,),
        "VALID",
        dimension_numbers=("NWC", "WIO", "NWC"),
        feature_group_count=taps.shape[1],
        precision=lax.Precision.HIGHEST,
    )


def extend_conv(rim, stream, taps):
    extended = jnp.concatenate([rim, stream], axis=0).astype(jnp.float32)[None]
    return causal_conv(extended, taps)[0]


def mode_weight(rate, res):
    return res * jnp.sqrt(-jnp.expm1(-2.0 * rate))


def carry_factor(rate_t, res_t, length):
    times = (jnp.arange(length) + 1).astype(jnp.float32)
    return mode_weight(rate_t, res_t)[:, :, None] * jnp.exp(
        -rate_t[:, :, None] * times[None, None, :]
    )


def inner_block(blocks, rate_g, res_g):
    width = blocks.shape[2]
    lag = jnp.arange(width)[:, None] - jnp.arange(width)[None, :]
    lagf = jnp.maximum(lag, 0).astype(jnp.float32)
    weight = mode_weight(rate_g, res_g)
    terms = weight[:, :, None, None] * jnp.exp(-rate_g[:, :, None, None] * lagf[None, None])
    toeplitz = jnp.where((lag >= 0)[None], jnp.sum(terms, axis=1), 0.0)
    return jnp.einsum("cbj,cij->cbi", blocks, toeplitz, precision=lax.Precision.HIGHEST)


def combine(earlier, later):
    return (earlier[0] * later[0], later[0] * earlier[1] + later[1])


def modal_long(values, rate, res):
    channels, length = values.shape
    width = 128
    count = length // width
    blocks = values.reshape(channels, count, width)
    rate_t = rate.T
    res_t = res.T
    group = min(channels, 16)
    groups = channels // group
    modes = rate_t.shape[1]

    def one_group(triple):
        return inner_block(triple[0], triple[1], triple[2])

    local = lax.map(
        one_group,
        (
            blocks.reshape(groups, group, count, width),
            rate_t.reshape(groups, group, modes),
            res_t.reshape(groups, group, modes),
        ),
    )
    local = local.reshape(channels, count, width)
    lags = (width - 1 - jnp.arange(width)).astype(jnp.float32)
    edge = jnp.exp(-rate_t[:, :, None] * lags[None, None, :])
    ends = jnp.einsum("cbj,cmj->cbm", blocks, edge, precision=lax.Precision.HIGHEST)
    decay = jnp.broadcast_to(jnp.exp(-rate_t * width)[:, None, :], ends.shape)
    _, inclusive = lax.associative_scan(combine, (decay, ends), axis=1)
    starts = jnp.concatenate([jnp.zeros_like(inclusive[:, :1]), inclusive[:, :-1]], axis=1)
    carried = jnp.einsum(
        "cbm,cmi->cbi", starts, carry_factor(rate_t, res_t, width), precision=lax.Precision.HIGHEST
    )
    return ((local + carried).reshape(channels, length), inclusive[:, -1])


def shards(q_mr, k_mr, v_mr, q_li, k_li, short_taps, mr_taps, norm_gain, decay_rate, residue):
    short_rim = short_taps.shape[1] - 1
    filt_rim = mr_taps.shape[0] - 1
    stacked = jnp.stack(
        [
            q_mr[-short_rim:],
            k_mr[-short_rim:],
            v_mr[-short_rim:],
            q_li[-short_rim:],
            k_li[-short_rim:],
        ]
    )
    rims = shifted(stacked, "ctx", 1)
    sq = extend_conv(rims[0], q_mr, short_taps[0])
    sk = extend_conv(rims[1], k_mr, short_taps[1])
    sv = extend_conv(rims[2], v_mr, short_taps[2])
    u_mr = settle(sk * sv)
    u_rim = shifted(u_mr[-filt_rim:], "ctx", 1)
    u_ext = jnp.concatenate([u_rim, u_mr], axis=0)
    query_rim, key_rim = (rims[3], rims[4])
    mr_long = causal_conv(u_ext.astype(jnp.float32)[None], mr_taps)[0]
    mixer_mr = (sq * mr_long).astype(jnp.bfloat16)
    wide = mixer_mr.astype(jnp.float32)
    totals = lax.psum(jnp.sum(wide * wide, axis=1), "mp")
    normed = settle(wide * lax.rsqrt(totals / D + 1e-06)[:, None] * norm_gain[None, :])
    value_rim = shifted(normed[-short_rim:], "ctx", 1)
    lq = extend_conv(query_rim, q_li, short_taps[3])
    lk = extend_conv(key_rim, k_li, short_taps[4])
    lv = extend_conv(value_rim, normed, short_taps[5])
    u_li = settle(lk * lv)
    owned = lax.all_to_all(u_li.T, "ctx", split_axis=0, concat_axis=1, tiled=True)
    narrow = owned.shape[0]
    first = lax.axis_index("ctx") * narrow
    own_rate = lax.dynamic_slice_in_dim(decay_rate, first, narrow, 1)
    own_res = lax.dynamic_slice_in_dim(residue, first, narrow, 1)
    result, _ = modal_long(owned.astype(jnp.float32), own_rate, own_res)
    long_own = settle(result)
    long_li = lax.all_to_all(long_own, "ctx", split_axis=1, concat_axis=0, tiled=True).T
    mixer_li = (lq * long_li.astype(jnp.float32)).astype(jnp.bfloat16)
    return (mixer_mr, mixer_li)


def solution(mesh):
    in_specs = (
        P("ctx", "mp"),
        P("ctx", "mp"),
        P("ctx", "mp"),
        P("ctx", "mp"),
        P("ctx", "mp"),
        P(None, None, "mp"),
        P(None, "mp"),
        P("mp"),
        P(None, "mp"),
        P(None, "mp"),
    )
    out_specs = (P("ctx", "mp"), P("ctx", "mp"))
    return jax.shard_map(shards, mesh=mesh, in_specs=in_specs, out_specs=out_specs, check_vma=False)
```

profile of v0, /device:TPU:32, one launch (start us, length us, event | category | flops | bytes accessed | tf_op | source)
XLA Modules:
  0.0 191.4 jit_solution(15018670686928462902)
XLA Ops:
  4.4 3.5 %collective-permute-start = (bf16[5,2,1024]{2,1,0:T(2,128)(2,1)S(1)}, bf16[5,2,1024]{2,1,0:T(2,128)(2,1)S(1)}, u32[]{:S(2)}, u32[]{:S(2)}) collective-permute-start(bf16[5,2,1024]{2,1,0:T(2,128)(2,1)S(1)} %constant_dynamic-update-slice_fusion), channel_id=1, source_target_pairs={{0,4},{4,8},{8,12},{12,16},{16,20},{20,24},{24,28},{28,32},{32,36}... | collective-permute-start | bytes 61448 | tf_op jit(solution)/shard_map/ppermute | solution.py:12
  7.9 1.4 slice_bitcast_fusion.3
  10.8 2.4 %rev.22 = f32[3,1024]{1,0:T(4,128)} reverse(f32[3,1024]{1,0:T(4,128)S(1)} %get-tuple-element.26), dimensions={0} | reverse | bytes 24576 | tf_op jit(solution)/shard_map/rev | solution.py:20
  13.2 2.4 %rev.23 = f32[3,1024]{1,0:T(4,128)} reverse(f32[3,1024]{1,0:T(4,128)S(1)} %get-tuple-element.25), dimensions={0} | reverse | bytes 24576 | tf_op jit(solution)/shard_map/rev | solution.py:20
  15.7 2.4 %rev.21 = f32[3,1024]{1,0:T(4,128)} reverse(f32[3,1024]{1,0:T(4,128)S(1)} %get-tuple-element.27), dimensions={0} | reverse | bytes 24576 | tf_op jit(solution)/shard_map/rev | solution.py:20
  18.1 4.7 %rev.24 = f32[128,1024]{1,0:T(8,128)} reverse(f32[128,1024]{1,0:T(8,128)} %param.16), dimensions={0} | reverse | bytes 1048576 | tf_op jit(solution)/shard_map/rev | solution.py:20
  22.8 2.4 %rev.26 = f32[3,1024]{1,0:T(4,128)} reverse(f32[3,1024]{1,0:T(4,128)S(1)} %get-tuple-element.28), dimensions={0} | reverse | bytes 24576 | tf_op jit(solution)/shard_map/rev | solution.py:20
  25.2 2.4 %rev.27 = f32[3,1024]{1,0:T(4,128)} reverse(f32[3,1024]{1,0:T(4,128)S(1)} %get-tuple-element.23), dimensions={0} | reverse | bytes 24576 | tf_op jit(solution)/shard_map/rev | solution.py:20
  34.6 3.5 %collective-permute-start.1 = (bf16[127,1024]{1,0:T(8,128)(2,1)}, bf16[127,1024]{1,0:T(8,128)(2,1)}, u32[]{:S(2)}, u32[]{:S(2)}) collective-permute-start(bf16[127,1024]{1,0:T(8,128)(2,1)} %slice.284), channel_id=1, source_target_pairs={{0,4},{4,8},{8,12},{12,16},{16,20},{20,24},{24,28},{28,32},{32,36}... | collective-permute-start | bytes 780296 | tf_op jit(solution)/shard_map/ppermute | solution.py:12
  39.7 1.3 reshape.135
  41.0 1.2 maximum_bitcast_fusion.5
  42.8 3.8 %collective-permute-done.1 = bf16[127,1024]{1,0:T(8,128)(2,1)} collective-permute-done((bf16[127,1024]{1,0:T(8,128)(2,1)}, bf16[127,1024]{1,0:T(8,128)(2,1)}, u32[]{:S(2)}, u32[]{:S(2)}) %collective-permute-start.1) | collective-permute-done | bytes 260128 | tf_op jit(solution)/shard_map/ppermute | solution.py:12
  46.6 1.1 maximum_bitcast_fusion
  47.7 11.1 %fusion.16 = bf16[1,256,1024]{2,0,1:T(2,128)(2,1)S(1)} fusion(bf16[1,383,1024]{2,1,0:T(8,128)(2,1)S(1)} %maximum_bitcast_fusion, f32[1,264,1024]{2,0,1:T(1,128)S(1)} %reshape.135, f32[128,1,1024]{2,0,1:T(8,128)S(1)} %bitcast.141), kind=kOutput, calls=%fused_computation.25 | convolution fusion | flops 403177472 | bytes 2881536 | tf_op jit(solution)/shard_map/conv_general_dilated | solution.py:21
  59.2 5.7 %psum.7 = f32[256]{0:T(256)S(1)} all-reduce(f32[256]{0:T(256)S(1)} %get-tuple-element.12), channel_id=1, replica_groups=mesh['ctx'=64,'mp'=4] {'mp'}, use_global_device_ids=true, to_apply=%region_1.0 | all-reduce | flops 256 | bytes 2048 | tf_op jit(solution)/shard_map/psum | solution.py:120
  65.1 1.9 %collective-permute-start.2 = (bf16[2,1024]{1,0:T(2,128)(2,1)S(1)}, bf16[2,1024]{1,0:T(2,128)(2,1)S(1)}, u32[]{:S(2)}, u32[]{:S(2)}) collective-permute-start(bf16[2,1024]{1,0:T(2,128)(2,1)S(1)} %slice.290), channel_id=1, source_target_pairs={{0,4},{4,8},{8,12},{12,16},{16,20},{20,24},{24,28},{28,32},{32,36}... | collective-permute-start | bytes 12296 | tf_op jit(solution)/shard_map/ppermute | solution.py:12
  67.0 1.3 convolution_select_fusion.1
  68.3 4.4 %collective-permute-done.2 = bf16[2,1024]{1,0:T(2,128)(2,1)S(1)} collective-permute-done((bf16[2,1024]{1,0:T(2,128)(2,1)S(1)}, bf16[2,1024]{1,0:T(2,128)(2,1)S(1)}, u32[]{:S(2)}, u32[]{:S(2)}) %collective-permute-start.2) | collective-permute-done | bytes 4128 | tf_op jit(solution)/shard_map/ppermute | solution.py:12
  75.0 1.0 copy.153
  76.0 14.2 %all-to-all-start = ((bf16[64,16,256]{2,1,0:T(8,128)(2,1)}), bf16[64,16,256]{2,1,0:T(8,128)(2,1)S(1)}, u32[]{:S(2)}, u32[]{:S(2)}) async-start(bf16[64,16,256]{2,1,0:T(8,128)(2,1)} %bitcast.40), calls=%async_computation | async-start | bytes 1048576 | tf_op jit(solution)/shard_map/all_to_all | solution.py:127
  91.4 4.3 %multiply_reduce_fusion = f32[16,128,128]{2,1,0:T(8,128)S(1)} fusion(f32[128,128]{1,0:T(8,128)S(1)} %maximum_convert_fusion, f32[16,16]{1,0:T(8,128)S(1)} %get-tuple-element.43, f32[16,16]{1,0:T(8,128)S(1)} %get-tuple-element.42), kind=kLoop, calls=%fused_computation | loop fusion | flops 12320768 | bytes 1116160 | tf_op jit(solution)/shard_map/while/body/eval_jaxpr/reduce_sum | solution.py:54
  95.7 13.1 %all-to-all-done = bf16[64,16,256]{2,1,0:T(8,128)(2,1)S(1)} async-done(((bf16[64,16,256]{2,1,0:T(8,128)(2,1)}), bf16[64,16,256]{2,1,0:T(8,128)(2,1)S(1)}, u32[]{:S(2)}, u32[]{:S(2)}) %all-to-all-start) | async-done | bytes 524320 | tf_op jit(solution)/shard_map/all_to_all | solution.py:127
  109.2 1.0 fusion.80
  110.1 2.3 %slice.223 = f32[16,64,16]{1,2,0:T(8,128)S(1)} slice(f32[16,128,16]{1,2,0:T(8,128)S(1)} %fusion.80), slice={[0:16:1], [0:127:2], [0:16:1]} | slice | bytes 131072 | tf_op jit(solution)/shard_map/slice | solution.py:89
  112.5 2.4 %slice.224 = f32[16,64,16]{1,2,0:T(8,128)S(1)} slice(f32[16,128,16]{1,2,0:T(8,128)S(1)} %fusion.80), slice={[0:16:1], [1:128:2], [0:16:1]} | slice | bytes 131072 | tf_op jit(solution)/shard_map/slice | solution.py:89
  115.0 1.2 slice.228
  116.2 1.3 slice.229
  122.5 1.0 slice.258
  123.5 1.3 slice.260
  124.8 1.8 slice.262
  126.6 2.9 %slice.264 = f32[16,63,16]{1,2,0:T(8,128)} slice(f32[16,128,16]{1,2,0:T(8,128)S(1)} %fusion.80), slice={[0:16:1], [2:128:2], [0:16:1]} | slice | bytes 129024 | tf_op jit(solution)/shard_map/slice | solution.py:89
  131.5 1.1 pad.46
  132.6 6.2 %pad.47 = f32[16,4,16]{1,2,0:T(8,128)S(1)} pad(f32[16,2,16]{1,2,0:T(8,128)} %pad_add_fusion, f32[]{:T(128)} %constant.47.clone.1), padding=0_0_0x1_0_1x0_0_0 | pad | bytes 6148 | tf_op jit(solution)/shard_map/pad | solution.py:89
  138.8 1.2 pad.49
  141.0 1.2 pad.48
  143.2 1.3 pad.50
  144.5 1.4 pad.51
  145.9 1.6 pad.53
  147.8 1.6 pad.52
  149.6 2.1 %pad.54 = f32[16,64,16]{1,2,0:T(8,128)S(1)} pad(f32[16,32,16]{1,2,0:T(8,128)S(1)} %pad_maximum_fusion.4, f32[]{:T(128)} %constant.47.clone.1), padding=0_0_0x0_1_1x0_0_0 | pad | bytes 98308 | tf_op jit(solution)/shard_map/pad | solution.py:89
  151.8 2.2 %pad.55 = f32[16,64,16]{1,2,0:T(8,128)S(1)} pad(f32[16,32,16]{1,2,0:T(8,128)S(1)} %add.135, f32[]{:T(128)} %constant.47.clone.1), padding=0_0_0x1_0_1x0_0_0 | pad | bytes 98308 | tf_op jit(solution)/shard_map/pad | solution.py:89
  154.0 3.2 %pad.195 = f32[16,128,16]{1,2,0:T(8,128)S(1)} pad(f32[16,64,16]{1,2,0:T(8,128)S(1)} %add.137, f32[]{:T(128)} %constant.47.clone.1), padding=0_0_0x1_0_1x0_0_0 | pad | bytes 196612
  157.4 3.4 %pad.115 = f32[16,127,16]{1,2,0:T(8,128)S(1)} pad(f32[16,64,16]{1,2,0:T(8,128)S(1)} %pad_maximum_fusion.5, f32[]{:T(128)} %constant.47.clone.1), padding=0_0_0x0_0_1x0_0_0 | pad | bytes 195588 | tf_op jit(solution)/shard_map/slice | solution.py:90
  160.9 1.2 fusion.24
  162.2 1.9 %fusion.6 = bf16[16,128,128]{2,1,0:T(8,128)(2,1)S(1)} fusion(f32[16,128,128]{2,1,0:T(8,128)S(1)} %fusion.24, f32[16,127,16]{1,2,0:T(8,128)S(1)} %slice_add_fusion.2, f32[128]{0:T(128)S(1)} %copy-done.35, f32[16,16]{1,0:T(8,128)S(1)} %copy-done.28, f32[16,16]{1,0:T(8,128)S(1)} %copy-done.16), kind=kOutput, calls=%fused_computation.16 | convolution fusion | flops 50921472 | bytes 1705472 | tf_op jit(solution)/shard_map/cbm,cmi->cbi/dot_general | solution.py:91
  165.3 5.5 %all-to-all-start.1 = ((bf16[16,64,256]{2,0,1:T(8,128)(2,1)}), bf16[16,64,256]{2,0,1:T(8,128)(2,1)}, u32[]{:S(2)}, u32[]{:S(2)}) async-start(bf16[16,64,256]{2,0,1:T(8,128)(2,1)} %bitcast.125), calls=%async_computation.1 | async-start | bytes 1048576 | tf_op jit(solution)/shard_map/all_to_all | solution.py:134
  172.9 16.0 %all-to-all-done.1 = bf16[16,64,256]{2,0,1:T(8,128)(2,1)} async-done(((bf16[16,64,256]{2,0,1:T(8,128)(2,1)}), bf16[16,64,256]{2,0,1:T(8,128)(2,1)}, u32[]{:S(2)}, u32[]{:S(2)}) %all-to-all-start.1) | async-done | bytes 524320 | tf_op jit(solution)/shard_map/all_to_all | solution.py:134
  188.9 1.2 convert_element_type.95
  (186 shorter events, 32.3 us)
Async XLA Ops:
  0.6 28.7 %copy-start.3 = (bf16[256,1024]{1,0:T(8,128)(2,1)S(1)}, bf16[256,1024]{1,0:T(8,128)(2,1)}, u32[]{:S(2)}) copy-start(bf16[256,1024]{1,0:T(8,128)(2,1)} %param.10) | copy-start | bytes 1572868
  0.6 28.7 %copy-start.4 = (bf16[256,1024]{1,0:T(8,128)(2,1)S(1)}, bf16[256,1024]{1,0:T(8,128)(2,1)}, u32[]{:S(2)}) copy-start(bf16[256,1024]{1,0:T(8,128)(2,1)} %param.11) | copy-start | bytes 1572868
  4.4 25.0 %collective-permute-start = (bf16[5,2,1024]{2,1,0:T(2,128)(2,1)S(1)}, bf16[5,2,1024]{2,1,0:T(2,128)(2,1)S(1)}, u32[]{:S(2)}, u32[]{:S(2)}) collective-permute-start(bf16[5,2,1024]{2,1,0:T(2,128)(2,1)S(1)} %constant_dynamic-update-slice_fusion), channel_id=1, source_target_pairs={{0,4},{4,8},{8,12},{12,16},{16,20},{20,24},{24,28},{28,32},{32,36}... | collective-permute-start | bytes 61448 | tf_op jit(solution)/shard_map/ppermute | solution.py:12
  10.8 104.1 %copy-start.17 = (f32[16,16]{1,0:T(8,128)}, f32[16,16]{1,0:T(8,128)S(1)}, u32[]{:S(2)}) copy-start(f32[16,16]{1,0:T(8,128)S(1)} %get-tuple-element.41) | copy-start | bytes 3076
  10.8 106.7 %copy-start.19 = (f32[16,16]{1,0:T(8,128)}, f32[16,16]{1,0:T(8,128)S(1)}, u32[]{:S(2)}) copy-start(f32[16,16]{1,0:T(8,128)S(1)} %get-tuple-element.38) | copy-start | bytes 3076
  10.8 108.3 %copy-start.21 = (f32[16,16]{1,0:T(8,128)}, f32[16,16]{1,0:T(8,128)S(1)}, u32[]{:S(2)}) copy-start(f32[16,16]{1,0:T(8,128)S(1)} %get-tuple-element.40) | copy-start | bytes 3076
  10.8 109.4 %copy-start.23 = (f32[16,16]{1,0:T(8,128)}, f32[16,16]{1,0:T(8,128)S(1)}, u32[]{:S(2)}) copy-start(f32[16,16]{1,0:T(8,128)S(1)} %get-tuple-element.39) | copy-start | bytes 3076
  10.8 110.1 %copy-start.24 = (f32[16,16]{1,0:T(8,128)}, f32[16,16]{1,0:T(8,128)S(1)}, u32[]{:S(2)}) copy-start(f32[16,16]{1,0:T(8,128)S(1)} %get-tuple-element.35) | copy-start | bytes 3076
  29.9 1.0 copy-start.5
  29.9 1.2 copy-start.6
  31.5 0.7 copy-start.33
  31.5 0.7 copy-start.36
  32.2 0.7 copy-start.32
  34.6 12.1 %collective-permute-start.1 = (bf16[127,1024]{1,0:T(8,128)(2,1)}, bf16[127,1024]{1,0:T(8,128)(2,1)}, u32[]{:S(2)}, u32[]{:S(2)}) collective-permute-start(bf16[127,1024]{1,0:T(8,128)(2,1)} %slice.284), channel_id=1, source_target_pairs={{0,4},{4,8},{8,12},{12,16},{16,20},{20,24},{24,28},{28,32},{32,36}... | collective-permute-start | bytes 780296 | tf_op jit(solution)/shard_map/ppermute | solution.py:12
  38.1 0.7 copy-start.31
  42.8 5.0 %copy-start.1 = (bf16[1,8,33,1024]{3,1,2,0:T(8,128)(2,1)}, bf16[1,8,33,1024]{3,1,2,0:T(8,128)(2,1)S(1)}, u32[]{:S(2)}) copy-start(bf16[1,8,33,1024]{3,1,2,0:T(8,128)(2,1)S(1)} %copy.147) | copy-start | bytes 1622020
  42.8 5.0 %copy-start.9 = (f32[128,1024]{1,0:T(8,128)S(1)}, f32[128,1024]{1,0:T(8,128)}, u32[]{:S(2)}) copy-start(f32[128,1024]{1,0:T(8,128)} %rev.24) | copy-start | bytes 1572868
  58.9 6.0 %copy-start.34 = (f32[1024]{0:T(1024)S(1)}, f32[1024]{0:T(1024)}, u32[]{:S(2)}) copy-start(f32[1024]{0:T(1024)} %param.17) | copy-start | bytes 12292
  58.9 8.1 %copy-start.2 = (bf16[1,8,33,1024]{3,1,2,0:T(8,128)(2,1)S(1)}, bf16[1,8,33,1024]{3,1,2,0:T(8,128)(2,1)}, u32[]{:S(2)}) copy-start(bf16[1,8,33,1024]{3,1,2,0:T(8,128)(2,1)} %copy-done.1) | copy-start | bytes 1622020
  58.9 8.1 %copy-start.30 = (f32[3,1024]{1,0:T(4,128)S(1)}, f32[3,1024]{1,0:T(4,128)}, u32[]{:S(2)}) copy-start(f32[3,1024]{1,0:T(4,128)} %rev.26) | copy-start | bytes 36868
  58.9 8.1 %copy-start.37 = (pred[8,33]{0,1:T(8,128)(4,1)S(1)}, pred[8,33]{0,1:T(8,128)(4,1)}, u32[]{:S(2)}) copy-start(pred[8,33]{0,1:T(8,128)(4,1)} %constant.113) | copy-start | bytes 796
  59.1 9.1 %copy-start = (bf16[256,1024]{1,0:T(8,128)(2,1)}, bf16[256,1024]{1,0:T(8,128)(2,1)S(1)}, u32[]{:S(2)}) copy-start(bf16[256,1024]{1,0:T(8,128)(2,1)S(1)} %get-tuple-element.13) | copy-start | bytes 1572868
  65.1 7.6 %collective-permute-start.2 = (bf16[2,1024]{1,0:T(2,128)(2,1)S(1)}, bf16[2,1024]{1,0:T(2,128)(2,1)S(1)}, u32[]{:S(2)}, u32[]{:S(2)}) collective-permute-start(bf16[2,1024]{1,0:T(2,128)(2,1)S(1)} %slice.290), channel_id=1, source_target_pairs={{0,4},{4,8},{8,12},{12,16},{16,20},{20,24},{24,28},{28,32},{32,36}... | collective-permute-start | bytes 12296 | tf_op jit(solution)/shard_map/ppermute | solution.py:12
  72.8 0.7 copy-start.29
  72.9 1.2 copy-start.39
  76.0 32.8 %all-to-all-start = ((bf16[64,16,256]{2,1,0:T(8,128)(2,1)}), bf16[64,16,256]{2,1,0:T(8,128)(2,1)S(1)}, u32[]{:S(2)}, u32[]{:S(2)}) async-start(bf16[64,16,256]{2,1,0:T(8,128)(2,1)} %bitcast.40), calls=%async_computation | async-start | bytes 1048576 | tf_op jit(solution)/shard_map/all_to_all | solution.py:127
  91.4 4.3 %copy-start.27 = (f32[16,16]{1,0:T(8,128)}, f32[16,16]{1,0:T(8,128)S(1)}, u32[]{:S(2)}) copy-start(f32[16,16]{1,0:T(8,128)S(1)} %get-tuple-element.42) | copy-start | bytes 3076
  91.4 17.7 %copy-start.15 = (f32[16,16]{1,0:T(8,128)}, f32[16,16]{1,0:T(8,128)S(1)}, u32[]{:S(2)}) copy-start(f32[16,16]{1,0:T(8,128)S(1)} %get-tuple-element.43) | copy-start | bytes 3076
  121.0 9.3 %copy-start.8 = (f32[16,1,16]{1,2,0:T(8,128)S(1)}, f32[16,1,16]{1,2,0:T(8,128)}, u32[]{:S(2)}) copy-start(f32[16,1,16]{1,2,0:T(8,128)} %copy.157) | copy-start | bytes 3076
  123.5 7.7 %copy-start.7 = (f32[16,1,16]{1,2,0:T(8,128)S(1)}, f32[16,1,16]{1,2,0:T(8,128)}, u32[]{:S(2)}) copy-start(f32[16,1,16]{1,2,0:T(8,128)} %copy.158) | copy-start | bytes 3076
  131.3 8.7 %copy-start.14 = (f32[16,3,16]{1,2,0:T(8,128)S(1)}, f32[16,3,16]{1,2,0:T(8,128)}, u32[]{:S(2)}) copy-start(f32[16,3,16]{1,2,0:T(8,128)} %slice.256) | copy-start | bytes 9220
  138.8 3.4 %copy-start.13 = (f32[16,7,16]{1,2,0:T(8,128)S(1)}, f32[16,7,16]{1,2,0:T(8,128)}, u32[]{:S(2)}) copy-start(f32[16,7,16]{1,2,0:T(8,128)} %slice.258) | copy-start | bytes 21508
  142.2 5.3 %copy-start.12 = (f32[16,15,16]{1,2,0:T(8,128)S(1)}, f32[16,15,16]{1,2,0:T(8,128)}, u32[]{:S(2)}) copy-start(f32[16,15,16]{1,2,0:T(8,128)} %slice.260) | copy-start | bytes 46084
  142.2 5.3 %copy-start.22 = (f32[16,16]{1,0:T(8,128)S(1)}, f32[16,16]{1,0:T(8,128)}, u32[]{:S(2)}) copy-start(f32[16,16]{1,0:T(8,128)} %copy-done.21) | copy-start | bytes 3076
  145.9 3.5 %copy-start.11 = (f32[16,31,16]{1,2,0:T(8,128)S(1)}, f32[16,31,16]{1,2,0:T(8,128)}, u32[]{:S(2)}) copy-start(f32[16,31,16]{1,2,0:T(8,128)} %slice.262) | copy-start | bytes 95236
  145.9 3.5 %copy-start.20 = (f32[16,16]{1,0:T(8,128)S(1)}, f32[16,16]{1,0:T(8,128)}, u32[]{:S(2)}) copy-start(f32[16,16]{1,0:T(8,128)} %copy-done.19) | copy-start | bytes 3076
  149.4 7.8 %copy-start.10 = (f32[16,63,16]{1,2,0:T(8,128)S(1)}, f32[16,63,16]{1,2,0:T(8,128)}, u32[]{:S(2)}) copy-start(f32[16,63,16]{1,2,0:T(8,128)} %slice.264) | copy-start | bytes 193540
  149.4 7.8 %copy-start.18 = (f32[16,16]{1,0:T(8,128)S(1)}, f32[16,16]{1,0:T(8,128)}, u32[]{:S(2)}) copy-start(f32[16,16]{1,0:T(8,128)} %copy-done.17) | copy-start | bytes 3076
  153.9 7.0 %copy-start.25 = (pred[128,128]{1,0:T(8,128)(4,1)S(1)}, pred[128,128]{1,0:T(8,128)(4,1)}, u32[]{:S(2)}) copy-start(pred[128,128]{1,0:T(8,128)(4,1)} %fusion.88) | copy-start | bytes 49156
  160.9 1.3 copy-start.16
  160.9 1.3 copy-start.28
  160.9 1.3 copy-start.35
  164.5 6.4 %copy-start.26 = (f32[3,1024]{1,0:T(4,128)S(1)}, f32[3,1024]{1,0:T(4,128)}, u32[]{:S(2)}) copy-start(f32[3,1024]{1,0:T(4,128)} %get-tuple-element.24) | copy-start | bytes 36868
  165.3 23.6 %all-to-all-start.1 = ((bf16[16,64,256]{2,0,1:T(8,128)(2,1)}), bf16[16,64,256]{2,0,1:T(8,128)(2,1)}, u32[]{:S(2)}, u32[]{:S(2)}) async-start(bf16[16,64,256]{2,0,1:T(8,128)(2,1)} %bitcast.125), calls=%async_computation.1 | async-start | bytes 1048576 | tf_op jit(solution)/shard_map/all_to_all | solution.py:134
  171.2 0.7 copy-start.38
where the time goes:
time: 193 us; the launch traced here: 191 us
  local copies, waits for them, and re-layouts  83.4 us (43%)
  waiting for transfers between devices  37.3 us (19%)
  starting transfers between devices  28.6 us (15%)
  matrix products  18 us (9%)
  other arithmetic  16.6 us (9%)
  blocking collectives  5.67 us (3%)
    slice x19, local copies, waits for them, and re-layouts, modal_long(): _, inclusive = lax.associative_scan(combine, (decay, ends), axis=1)  20.3 us
    pad x10, local copies, waits for them, and re-layouts, modal_long(): _, inclusive = lax.associative_scan(combine, (decay, ends), axis=1)  19.9 us
    rev x7, local copies, waits for them, and re-layouts, causal_conv(): kernel = taps[::-1][:, None, :]  17.1 us
    all_to_all x1, waiting for transfers between devices, shards(): lax.all_to_all(long_own, 'ctx', split_axis=1, concat_axis=0, tiled=True)  16 us
    all_to_all x1, starting transfers between devices, shards(): lax.all_to_all(u_li.T, 'ctx', split_axis=0, concat_axis=1, tiled=True)  14.2 us
    conv_general_dilated x7, matrix products, causal_conv(): lax.conv_general_dilated(extended, kernel, (1,), 'VALID', dimension_numbe...  13.9 us
    all_to_all x1, waiting for transfers between devices, shards(): lax.all_to_all(u_li.T, 'ctx', split_axis=0, concat_axis=1, tiled=True)  13.1 us
    unnamed x88, local copies, waits for them, and re-layouts  9.39 us
  transfers between devices with their start and end apart: 5, of which 4 were waited for; matrix products, arithmetic and copies ran while one was open for 18% of the time, Pallas kernels for 0%

commit v1 on v0

v1 whole, which is shorter than its diff:
```python
import jax
import jax.numpy as jnp
from jax import lax
from jax.experimental import pallas as pl
from jax.experimental.pallas import tpu as pltpu
from jax.sharding import PartitionSpec as P

def shifted(shard, axis, by):
    devices = lax.axis_size(axis)
    pairs = [(i, i + by) for i in range(devices) if 0 <= i + by < devices]
    return lax.ppermute(shard, axis, pairs)


def to_bf16(values):
    return lax.reduce_precision(values, exponent_bits=8, mantissa_bits=7)


def short_conv(extended, taps, length):
    width = taps.shape[0]
    x = extended.astype(jnp.float32)
    total = taps[0][None, :] * x[width - 1 : width - 1 + length]
    for lag in range(1, width):
        start = width - 1 - lag
        total = total + taps[lag][None, :] * x[start : start + length]
    return total


def long_conv(extended, taps):
    kernel = taps[::-1][:, None, :]
    return lax.conv_general_dilated(
        extended[None],
        kernel,
        (1,),
        "VALID",
        dimension_numbers=("NWC", "WIO", "NWC"),
        feature_group_count=taps.shape[1],
        precision=lax.Precision.HIGHEST,
    )[0]


def mode_weight(rate, res):
    return res * jnp.sqrt(-jnp.expm1(-2.0 * rate))


def carry_in(ends, rate, width):
    devices = lax.axis_size("ctx")
    radix = 4
    state = shifted(ends, "ctx", 1)
    for j in range(2, radix + 1):
        if j < devices:
            state = state + jnp.exp(-width * (j - 1) * rate) * shifted(ends, "ctx", j)
    span = radix
    while span < devices:
        total = state
        for j in range(1, radix):
            if j * span < devices:
                total = total + jnp.exp(-width * (j * span) * rate) * shifted(state, "ctx", j * span)
        state = total
        span *= radix
    return state


LANES = 512


def _recur_body(u_ref, a_ref, w_ref, s0_ref, y_ref, end_ref):
    tokens, channels = u_ref.shape
    modes = a_ref.shape[0]
    for c0 in range(0, channels, LANES):
        cols = pl.ds(c0, LANES)
        a = a_ref[:, cols]
        w = w_ref[:, cols] if w_ref is not None else None

        def step(t, state):
            row = u_ref[pl.ds(t, 1), cols]
            state = a * state + row
            if y_ref is not None:
                y_ref[pl.ds(t, 1), cols] = jnp.sum(w * state, axis=0, keepdims=True)
            return state

        init = s0_ref[:, cols] if s0_ref is not None else jnp.zeros(a.shape, jnp.float32)
        state = lax.fori_loop(0, tokens, step, init, unroll=8)
        if end_ref is not None:
            end_ref[:, cols] = state


def _ends_kernel(u_ref, a_ref, end_ref):
    _recur_body(u_ref, a_ref, None, None, None, end_ref)


def _output_kernel(u_ref, a_ref, w_ref, s0_ref, y_ref):
    _recur_body(u_ref, a_ref, w_ref, s0_ref, y_ref, None)


def _vmem():
    return pl.BlockSpec(memory_space=pltpu.VMEM)


def recur_ends(u, a):
    tokens, channels = u.shape
    modes = a.shape[0]
    return pl.pallas_call(
        _ends_kernel,
        out_shape=jax.ShapeDtypeStruct(a.shape, jnp.float32),
        in_specs=[_vmem(), _vmem()],
        out_specs=_vmem(),
        cost_estimate=pl.CostEstimate(
            flops=2 * tokens * modes * channels, bytes_accessed=4 * (tokens + 2 * modes) * channels, transcendentals=0
        ),
    )(u, a)


def recur_output(u, a, w, s0):
    tokens, channels = u.shape
    modes = a.shape[0]
    return pl.pallas_call(
        _output_kernel,
        out_shape=jax.ShapeDtypeStruct(u.shape, jnp.float32),
        in_specs=[_vmem(), _vmem(), _vmem(), _vmem()],
        out_specs=_vmem(),
        cost_estimate=pl.CostEstimate(
            flops=4 * tokens * modes * channels, bytes_accessed=4 * (2 * tokens + 3 * modes) * channels, transcendentals=0
        ),
    )(u, a, w, s0)


def modal_long(u, rate, res):
    tokens = u.shape[0]
    weight = mode_weight(rate, res)
    a = jnp.exp(-rate)
    device_end = recur_ends(u, a)
    start_in = carry_in(device_end, rate, tokens)
    return recur_output(u, a, weight, start_in)


def shards(q_mr, k_mr, v_mr, q_li, k_li, short_taps, mr_taps, norm_gain, decay_rate, residue):
    tokens = q_mr.shape[0]
    width = short_taps.shape[1]
    short_rim = width - 1
    filt = mr_taps.shape[0]
    u_rows = filt - 1 + short_rim
    pack = 16
    sent_rows = -(-u_rows // pack) * pack
    tail = slice(tokens - sent_rows - short_rim, tokens)
    sk_tail = short_conv(k_mr[tail], short_taps[1], sent_rows)
    sv_tail = short_conv(v_mr[tail], short_taps[2], sent_rows)
    u_tail = (sk_tail * sv_tail).astype(jnp.bfloat16)
    q_rows = 2 * short_rim
    rims = [
        q_mr[tokens - q_rows :],
        k_mr[tokens - short_rim :],
        v_mr[tokens - short_rim :],
        q_li[tokens - short_rim :],
        k_li[tokens - short_rim :],
    ]
    small_rows = sum(r.shape[0] for r in rims)
    fill = jnp.zeros((-(-small_rows // pack) * pack - small_rows, q_mr.shape[1]), q_mr.dtype)
    got = shifted(jnp.concatenate([u_tail, jnp.concatenate(rims + [fill])]), "ctx", 1)
    u_rim = got[sent_rows - u_rows : sent_rows]
    at = sent_rows
    q_rim = got[at : at + q_rows]
    at += q_rows
    k_rim = got[at : at + short_rim]
    at += short_rim
    v_rim = got[at : at + short_rim]
    at += short_rim
    ql_rim = got[at : at + short_rim]
    at += short_rim
    kl_rim = got[at : at + short_rim]

    sk = short_conv(jnp.concatenate([k_rim, k_mr]), short_taps[1], tokens)
    sv = short_conv(jnp.concatenate([v_rim, v_mr]), short_taps[2], tokens)
    u_mr = (sk * sv).astype(jnp.bfloat16)
    u_ext = jnp.concatenate([u_rim, u_mr]).astype(jnp.float32)
    ext_rows = tokens + short_rim
    mr_long = long_conv(u_ext, mr_taps)
    sq = short_conv(jnp.concatenate([q_rim, q_mr]), short_taps[0], ext_rows)
    mixer_ext = to_bf16(sq * mr_long)
    mixer_mr = mixer_ext[short_rim:].astype(jnp.bfloat16)
    channels_all = mixer_ext.shape[1] * lax.axis_size("mp")
    totals = lax.psum(jnp.sum(mixer_ext * mixer_ext, axis=1), "mp")
    normed = to_bf16(mixer_ext * lax.rsqrt(totals / channels_all + 1e-06)[:, None] * norm_gain[None, :])
    lq = short_conv(jnp.concatenate([ql_rim, q_li]), short_taps[3], tokens)
    lk = short_conv(jnp.concatenate([kl_rim, k_li]), short_taps[4], tokens)
    lv = short_conv(normed, short_taps[5], tokens)
    u_li = to_bf16(lk * lv)
    long_li = to_bf16(modal_long(u_li, decay_rate, residue))
    mixer_li = (lq * long_li).astype(jnp.bfloat16)
    return (mixer_mr, mixer_li)


def solution(mesh):
    in_specs = (
        P("ctx", "mp"),
        P("ctx", "mp"),
        P("ctx", "mp"),
        P("ctx", "mp"),
        P("ctx", "mp"),
        P(None, None, "mp"),
        P(None, "mp"),
        P("mp"),
        P(None, "mp"),
        P(None, "mp"),
    )
    out_specs = (P("ctx", "mp"), P("ctx", "mp"))
    return jax.shard_map(shards, mesh=mesh, in_specs=in_specs, out_specs=out_specs, check_vma=False)
```

time: 193 us -> 110 us (0.57)
  the two profiles are of different devices: /device:TPU:32 before, /device:TPU:6 now
where the time goes in v1:
time: 110 us; the launch traced here: 109 us
  waiting for transfers between devices  40.2 us (37%)
  starting transfers between devices  24 us (22%)
  matrix products  11 us (10%)
  Pallas kernels  9.97 us (9%)
  other arithmetic  9.53 us (9%)
  local copies, waits for them, and re-layouts  8.06 us (7%)
  blocking collectives  5.77 us (5%)
    ppermute x11, waiting for transfers between devices, shifted(): return lax.ppermute(shard, axis, pairs)  40.2 us
    ppermute x11, starting transfers between devices, shifted(): return lax.ppermute(shard, axis, pairs)  24 us
    conv_general_dilated x1, matrix products, long_conv(): lax.conv_general_dilated(extended[None], kernel, (1,), 'VALID', dimension...  11 us
    pallas_call x1, Pallas kernels, recur_output(): pl.pallas_call(_output_kernel, out_shape=jax.ShapeDtypeStruct(u.shape, jn...  6.77 us
    psum x1, blocking collectives, shards(): totals = lax.psum(jnp.sum(mixer_ext * mixer_ext, axis=1), 'mp')  5.77 us
    pallas_call x1, Pallas kernels, recur_ends(): pl.pallas_call(_ends_kernel, out_shape=jax.ShapeDtypeStruct(a.shape, jnp....  3.19 us
    rev x1, local copies, waits for them, and re-layouts, long_conv(): kernel = taps[::-1][:, None, :]  2.62 us
    convert_element_type x1, other arithmetic, shards(): mixer_li = (lq * long_li).astype(jnp.bfloat16)  2.41 us
  transfers between devices with their start and end apart: 11, of which 9 were waited for; matrix products, arithmetic and copies ran while one was open for 4% of the time, Pallas kernels for 0%

profile of v1, /device:TPU:6, one launch (start us, length us, event | category | flops | bytes accessed | tf_op | source)
XLA Modules:
  0.0 109.5 jit_solution(4196618534080168922)
XLA Ops:
  0.7 0.8 slice.235
  1.5 1.2 %slice_convert_fusion.1 = (f32[146,1024]{1,0:T(8,128)S(1)}, f32[146,1024]{1,0:T(8,128)S(1)}) fusion(bf16[256,1024]{1,0:T(8,128)(2,1)} %param.12, bf16[256,1024]{1,0:T(8,128)(2,1)} %param.11), kind=kLoop, calls=%fused_computation.62 | loop fusion | flops 299008 | bytes 1794048 | tf_op jit(solution)/shard_map/convert_element_type | solution.py:20
  2.8 0.1 fusion.31
  2.9 0.7 slice.237
  3.6 0.4 fusion.24
  4.1 0.2 concatenate.21
  4.2 3.5 %collective-permute-start = (bf16[160,1024]{1,0:T(8,128)(2,1)S(1)}, bf16[160,1024]{1,0:T(8,128)(2,1)}, u32[]{:S(2)}, u32[]{:S(2)}) collective-permute-start(bf16[160,1024]{1,0:T(8,128)(2,1)S(1)} %concatenate.21), channel_id=1, source_target_pairs={{0,4},{4,8},{8,12},{12,16},{16,20},{20,24},{24,28},{28,32},{32,36}... | collective-permute-start | bytes 983048 | tf_op jit(solution)/shard_map/ppermute | solution.py:11
  7.7 2.6 %rev.3 = f32[128,1024]{1,0:T(8,128)} reverse(f32[128,1024]{1,0:T(8,128)S(1)} %copy-done.6), dimensions={0} | reverse | bytes 1048576 | tf_op jit(solution)/shard_map/rev | solution.py:29
  10.4 0.6 negate_exponential_fusion.a_ref
  11.0 12.1 %collective-permute-done = bf16[160,1024]{1,0:T(8,128)(2,1)} collective-permute-done((bf16[160,1024]{1,0:T(8,128)(2,1)S(1)}, bf16[160,1024]{1,0:T(8,128)(2,1)}, u32[]{:S(2)}, u32[]{:S(2)}) %collective-permute-start) | collective-permute-done | bytes 327712 | tf_op jit(solution)/shard_map/ppermute | solution.py:11
  23.1 0.8 fusion.30
  23.9 0.1 maximum_convert_fusion.1
  24.1 0.1 maximum_convert_fusion.2
  24.2 0.7 slice.281
  25.0 0.1 maximum_convert_fusion
  25.1 0.7 fusion.18
  25.8 1.1 slice.285
  26.9 0.1 maximum_bitcast_fusion
  27.1 11.0 %fusion = f32[1,258,1024]{2,0,1:T(1,128)S(1)} fusion(bf16[1,385,1024]{2,1,0:T(8,128)(2,1)S(1)} %maximum_bitcast_fusion, f32[128,1,1024]{2,0,1:T(8,128)S(1)} %bitcast.24), kind=kOutput, calls=%fused_computation | convolution fusion | flops 405798912 | bytes 2369536 | tf_op jit(solution)/shard_map/conv_general_dilated | solution.py:30
  38.0 0.7 multiply_reduce_fusion
  38.7 5.8 %psum.7 = f32[258]{0:T(512)S(1)} all-reduce(f32[258]{0:T(512)S(1)} %get-tuple-element.2), channel_id=1, replica_groups=mesh['ctx'=64,'mp'=4] {'mp'}, use_global_device_ids=true, to_apply=%region_1.0 | all-reduce | flops 258 | bytes 2064 | tf_op jit(solution)/shard_map/psum | solution.py:181
  44.5 0.1 maximum_convert_fusion.4
  44.7 0.2 multiply_reduce-precision_fusion
  44.9 1.7 %fusion.8.u_ref = f32[256,1024]{1,0:T(8,128)} fusion(f32[258,1024]{1,0:T(8,128)S(1)} %multiply_reduce-precision_fusion, f32[258,1024]{1,0:T(8,128)S(1)} %maximum_convert_fusion.4, f32[1024]{0:T(1024)S(1)} %bitcast.41, f32[1024]{0:T(1024)S(1)} %bitcast.42, f32[1024]{0:T(1024)S(1)} %bitcast.37, f32[1024]{0:T(1024)S(1)} %bitcast.38, f32[1024]{0:T(1024)S(1)} %bitcast.39, ...), kind=kLoop, calls=%fused_computation.14 | loop fusion | flops 3145728 | bytes 7364608 | tf_op jit(solution)/shard_map/reduce_precision | solution.py:15
  46.5 3.2 %shard_map.113 = f32[16,1024]{1,0:T(8,128)} custom-call(f32[256,1024]{1,0:T(8,128)} %fusion.8.u_ref, f32[16,1024]{1,0:T(8,128)} %negate_exponential_fusion.a_ref), custom_call_target="tpu_custom_call" | custom-call | flops 8388608 | bytes 1179648 | tf_op jit(solution)/shard_map/pallas_call | solution.py:102
  49.7 1.9 %collective-permute-start.1 = (f32[16,1024]{1,0:T(8,128)}, f32[16,1024]{1,0:T(8,128)S(1)}, u32[]{:S(2)}, u32[]{:S(2)}) collective-permute-start(f32[16,1024]{1,0:T(8,128)} %shard_map.113), channel_id=1, source_target_pairs={{0,4},{4,8},{8,12},{12,16},{16,20},{20,24},{24,28},{28,32},{32,36}... | collective-permute-start | bytes 196616 | tf_op jit(solution)/shard_map/ppermute | solution.py:11
  51.6 1.9 %collective-permute-start.2 = (f32[16,1024]{1,0:T(8,128)}, f32[16,1024]{1,0:T(8,128)S(1)}, u32[]{:S(2)}, u32[]{:S(2)}) collective-permute-start(f32[16,1024]{1,0:T(8,128)} %shard_map.113), channel_id=1, source_target_pairs={{0,8},{4,12},{8,16},{12,20},{16,24},{20,28},{24,32},{28,36},{32,40... | collective-permute-start | bytes 196616 | tf_op jit(solution)/shard_map/ppermute | solution.py:11
  53.6 1.9 %collective-permute-start.3 = (f32[16,1024]{1,0:T(8,128)}, f32[16,1024]{1,0:T(8,128)S(1)}, u32[]{:S(2)}, u32[]{:S(2)}) collective-permute-start(f32[16,1024]{1,0:T(8,128)} %shard_map.113), channel_id=1, source_target_pairs={{0,12},{4,16},{8,20},{12,24},{16,28},{20,32},{24,36},{28,40},{32,4... | collective-permute-start | bytes 196616 | tf_op jit(solution)/shard_map/ppermute | solution.py:11
  55.5 3.5 %collective-permute-start.4 = (f32[16,1024]{1,0:T(8,128)}, f32[16,1024]{1,0:T(8,128)S(1)}, u32[]{:S(2)}, u32[]{:S(2)}) collective-permute-start(f32[16,1024]{1,0:T(8,128)} %shard_map.113), channel_id=1, source_target_pairs={{0,16},{4,20},{8,24},{12,28},{16,32},{20,36},{24,40},{28,44},{32,4... | collective-permute-start | bytes 196616 | tf_op jit(solution)/shard_map/ppermute | solution.py:11
  59.0 2.8 %collective-permute-done.1 = f32[16,1024]{1,0:T(8,128)S(1)} collective-permute-done((f32[16,1024]{1,0:T(8,128)}, f32[16,1024]{1,0:T(8,128)S(1)}, u32[]{:S(2)}, u32[]{:S(2)}) %collective-permute-start.1) | collective-permute-done | bytes 65568 | tf_op jit(solution)/shard_map/ppermute | solution.py:11
  61.8 2.2 %collective-permute-done.2 = f32[16,1024]{1,0:T(8,128)S(1)} collective-permute-done((f32[16,1024]{1,0:T(8,128)}, f32[16,1024]{1,0:T(8,128)S(1)}, u32[]{:S(2)}, u32[]{:S(2)}) %collective-permute-start.2) | collective-permute-done | bytes 65568 | tf_op jit(solution)/shard_map/ppermute | solution.py:11
  64.0 2.7 %collective-permute-done.3 = f32[16,1024]{1,0:T(8,128)S(1)} collective-permute-done((f32[16,1024]{1,0:T(8,128)}, f32[16,1024]{1,0:T(8,128)S(1)}, u32[]{:S(2)}, u32[]{:S(2)}) %collective-permute-start.3) | collective-permute-done | bytes 65568 | tf_op jit(solution)/shard_map/ppermute | solution.py:11
  66.8 1.4 %collective-permute-done.4 = f32[16,1024]{1,0:T(8,128)S(1)} collective-permute-done((f32[16,1024]{1,0:T(8,128)}, f32[16,1024]{1,0:T(8,128)S(1)}, u32[]{:S(2)}, u32[]{:S(2)}) %collective-permute-start.4) | collective-permute-done | bytes 65568 | tf_op jit(solution)/shard_map/ppermute | solution.py:11
  68.2 1.9 %collective-permute-start.5 = (f32[16,1024]{1,0:T(8,128)S(1)}, f32[16,1024]{1,0:T(8,128)S(1)}, u32[]{:S(2)}, u32[]{:S(2)}) collective-permute-start(f32[16,1024]{1,0:T(8,128)S(1)} %multiply_add_fusion.2), channel_id=1, source_target_pairs={{0,16},{4,20},{8,24},{12,28},{16,32},{20,36},{24,40},{28,44},{32,4... | collective-permute-start | bytes 196616 | tf_op jit(solution)/shard_map/ppermute | solution.py:11
  70.1 2.4 %collective-permute-start.6 = (f32[16,1024]{1,0:T(8,128)S(1)}, f32[16,1024]{1,0:T(8,128)S(1)}, u32[]{:S(2)}, u32[]{:S(2)}) collective-permute-start(f32[16,1024]{1,0:T(8,128)S(1)} %multiply_add_fusion.2), channel_id=1, source_target_pairs={{0,32},{4,36},{8,40},{12,44},{16,48},{20,52},{24,56},{28,60},{32,6... | collective-permute-start | bytes 196616 | tf_op jit(solution)/shard_map/ppermute | solution.py:11
  72.5 3.1 %collective-permute-start.7 = (f32[16,1024]{1,0:T(8,128)S(1)}, f32[16,1024]{1,0:T(8,128)S(1)}, u32[]{:S(2)}, u32[]{:S(2)}) collective-permute-start(f32[16,1024]{1,0:T(8,128)S(1)} %multiply_add_fusion.2), channel_id=1, source_target_pairs={{0,48},{4,52},{8,56},{12,60},{16,64},{20,68},{24,72},{28,76},{32,8... | collective-permute-start | bytes 196616 | tf_op jit(solution)/shard_map/ppermute | solution.py:11
  75.6 3.3 %collective-permute-done.5 = f32[16,1024]{1,0:T(8,128)S(1)} collective-permute-done((f32[16,1024]{1,0:T(8,128)S(1)}, f32[16,1024]{1,0:T(8,128)S(1)}, u32[]{:S(2)}, u32[]{:S(2)}) %collective-permute-start.5) | collective-permute-done | bytes 65568 | tf_op jit(solution)/shard_map/ppermute | solution.py:11
  79.0 5.1 %collective-permute-done.6 = f32[16,1024]{1,0:T(8,128)S(1)} collective-permute-done((f32[16,1024]{1,0:T(8,128)S(1)}, f32[16,1024]{1,0:T(8,128)S(1)}, u32[]{:S(2)}, u32[]{:S(2)}) %collective-permute-start.6) | collective-permute-done | bytes 65568 | tf_op jit(solution)/shard_map/ppermute | solution.py:11
  84.1 1.6 %collective-permute-done.7 = f32[16,1024]{1,0:T(8,128)S(1)} collective-permute-done((f32[16,1024]{1,0:T(8,128)S(1)}, f32[16,1024]{1,0:T(8,128)S(1)}, u32[]{:S(2)}, u32[]{:S(2)}) %collective-permute-start.7) | collective-permute-done | bytes 65568 | tf_op jit(solution)/shard_map/ppermute | solution.py:11
  85.7 0.7 collective-permute-start.10
  86.4 1.9 %collective-permute-start.8 = (f32[16,1024]{1,0:T(8,128)S(1)}, f32[16,1024]{1,0:T(8,128)S(1)}, u32[]{:S(2)}, u32[]{:S(2)}) collective-permute-start(f32[16,1024]{1,0:T(8,128)S(1)} %multiply_add_fusion.1), channel_id=1, source_target_pairs={{0,64},{4,68},{8,72},{12,76},{16,80},{20,84},{24,88},{28,92},{32,9... | collective-permute-start | bytes 196616 | tf_op jit(solution)/shard_map/ppermute | solution.py:11
  88.3 1.3 %collective-permute-start.9 = (f32[16,1024]{1,0:T(8,128)S(1)}, f32[16,1024]{1,0:T(8,128)S(1)}, u32[]{:S(2)}, u32[]{:S(2)}) collective-permute-start(f32[16,1024]{1,0:T(8,128)S(1)} %multiply_add_fusion.1), channel_id=1, source_target_pairs={{0,128},{4,132},{8,136},{12,140},{16,144},{20,148},{24,152},{28,15... | collective-permute-start | bytes 196616 | tf_op jit(solution)/shard_map/ppermute | solution.py:11
  89.6 0.1 maximum_convert_fusion.3
  89.8 0.9 slice.423
  90.7 8.8 %collective-permute-done.8 = f32[16,1024]{1,0:T(8,128)S(1)} collective-permute-done((f32[16,1024]{1,0:T(8,128)S(1)}, f32[16,1024]{1,0:T(8,128)S(1)}, u32[]{:S(2)}, u32[]{:S(2)}) %collective-permute-start.8) | collective-permute-done | bytes 65568 | tf_op jit(solution)/shard_map/ppermute | solution.py:11
  99.5 0.7 multiply_add_fusion
  100.3 6.8 %shard_map.114 = f32[256,1024]{1,0:T(8,128)} custom-call(f32[256,1024]{1,0:T(8,128)} %fusion.8.u_ref, f32[16,1024]{1,0:T(8,128)} %negate_exponential_fusion.a_ref, f32[16,1024]{1,0:T(8,128)} %get-tuple-element.27.w_ref, f32[16,1024]{1,0:T(8,128)} %get-tuple-element.26.s0_ref), custom_call_target="tpu_custom_call" | custom-call | flops 16777216 | bytes 2293760 | tf_op jit(solution)/shard_map/pallas_call | solution.py:116
  107.0 2.4 %fusion.14 = bf16[256,1024]{1,0:T(8,128)(2,1)} fusion(f32[258,1024]{1,0:T(8,128)S(1)} %maximum_convert_fusion.3, f32[256,1024]{1,0:T(8,128)} %shard_map.114, f32[1024]{0:T(1024)S(1)} %bitcast.44, f32[1024]{0:T(1024)S(1)} %bitcast.45, f32[1024]{0:T(1024)S(1)} %bitcast.43), kind=kLoop, calls=%fused_computation.26 | loop fusion | flops 2097152 | bytes 4730880 | tf_op jit(solution)/shard_map/convert_element_type | solution.py:188
  (31 shorter events, 0.2 us)
Async XLA Ops:
  0.6 2.1 %copy-start.1 = (bf16[256,1024]{1,0:T(8,128)(2,1)S(1)}, bf16[256,1024]{1,0:T(8,128)(2,1)}, u32[]{:S(2)}) copy-start(bf16[256,1024]{1,0:T(8,128)(2,1)} %param.12) | copy-start | bytes 1572868
  0.6 2.1 %copy-start.9 = (f32[6,3,1024]{2,1,0:T(4,128)S(1)}, f32[6,3,1024]{2,1,0:T(4,128)}, u32[]{:S(2)}) copy-start(f32[6,3,1024]{2,1,0:T(4,128)} %param.15) | copy-start | bytes 221188
  0.7 2.2 %copy-start.3 = (bf16[256,1024]{1,0:T(8,128)(2,1)S(1)}, bf16[256,1024]{1,0:T(8,128)(2,1)}, u32[]{:S(2)}) copy-start(bf16[256,1024]{1,0:T(8,128)(2,1)} %param.10) | copy-start | bytes 1572868
  0.7 2.9 %copy-start.4 = (bf16[256,1024]{1,0:T(8,128)(2,1)S(1)}, bf16[256,1024]{1,0:T(8,128)(2,1)}, u32[]{:S(2)}) copy-start(bf16[256,1024]{1,0:T(8,128)(2,1)} %param.14) | copy-start | bytes 1572868
  3.6 4.1 %copy-start.6 = (f32[128,1024]{1,0:T(8,128)S(1)}, f32[128,1024]{1,0:T(8,128)}, u32[]{:S(2)}) copy-start(f32[128,1024]{1,0:T(8,128)} %param.16) | copy-start | bytes 1572868
  4.0 6.3 %copy-start.2 = (f32[16,1024]{1,0:T(8,128)S(1)}, f32[16,1024]{1,0:T(8,128)}, u32[]{:S(2)}) copy-start(f32[16,1024]{1,0:T(8,128)} %param.18) | copy-start | bytes 196612
  4.0 19.9 %copy-start = (bf16[256,1024]{1,0:T(8,128)(2,1)S(1)}, bf16[256,1024]{1,0:T(8,128)(2,1)}, u32[]{:S(2)}) copy-start(bf16[256,1024]{1,0:T(8,128)(2,1)} %param.11) | copy-start | bytes 1572868
  4.2 18.9 %collective-permute-start = (bf16[160,1024]{1,0:T(8,128)(2,1)S(1)}, bf16[160,1024]{1,0:T(8,128)(2,1)}, u32[]{:S(2)}, u32[]{:S(2)}) collective-permute-start(bf16[160,1024]{1,0:T(8,128)(2,1)S(1)} %concatenate.21), channel_id=1, source_target_pairs={{0,4},{4,8},{8,12},{12,16},{16,20},{20,24},{24,28},{28,32},{32,36}... | collective-permute-start | bytes 983048 | tf_op jit(solution)/shard_map/ppermute | solution.py:11
  25.8 1.3 %copy-start.7 = (f32[128,1024]{1,0:T(8,128)S(1)}, f32[128,1024]{1,0:T(8,128)}, u32[]{:S(2)}) copy-start(f32[128,1024]{1,0:T(8,128)} %rev.3) | copy-start | bytes 1572868
  38.7 5.9 %copy-start.10 = (f32[1024]{0:T(1024)S(1)}, f32[1024]{0:T(1024)}, u32[]{:S(2)}) copy-start(f32[1024]{0:T(1024)} %param.17) | copy-start | bytes 12292
  46.5 43.1 %copy-start.5 = (bf16[256,1024]{1,0:T(8,128)(2,1)S(1)}, bf16[256,1024]{1,0:T(8,128)(2,1)}, u32[]{:S(2)}) copy-start(bf16[256,1024]{1,0:T(8,128)(2,1)} %param.13) | copy-start | bytes 1572868
  49.7 12.1 %collective-permute-start.1 = (f32[16,1024]{1,0:T(8,128)}, f32[16,1024]{1,0:T(8,128)S(1)}, u32[]{:S(2)}, u32[]{:S(2)}) collective-permute-start(f32[16,1024]{1,0:T(8,128)} %shard_map.113), channel_id=1, source_target_pairs={{0,4},{4,8},{8,12},{12,16},{16,20},{20,24},{24,28},{28,32},{32,36}... | collective-permute-start | bytes 196616 | tf_op jit(solution)/shard_map/ppermute | solution.py:11
  51.6 12.4 %collective-permute-start.2 = (f32[16,1024]{1,0:T(8,128)}, f32[16,1024]{1,0:T(8,128)S(1)}, u32[]{:S(2)}, u32[]{:S(2)}) collective-permute-start(f32[16,1024]{1,0:T(8,128)} %shard_map.113), channel_id=1, source_target_pairs={{0,8},{4,12},{8,16},{12,20},{16,24},{20,28},{24,32},{28,36},{32,40... | collective-permute-start | bytes 196616 | tf_op jit(solution)/shard_map/ppermute | solution.py:11
  53.6 13.2 %collective-permute-start.3 = (f32[16,1024]{1,0:T(8,128)}, f32[16,1024]{1,0:T(8,128)S(1)}, u32[]{:S(2)}, u32[]{:S(2)}) collective-permute-start(f32[16,1024]{1,0:T(8,128)} %shard_map.113), channel_id=1, source_target_pairs={{0,12},{4,16},{8,20},{12,24},{16,28},{20,32},{24,36},{28,40},{32,4... | collective-permute-start | bytes 196616 | tf_op jit(solution)/shard_map/ppermute | solution.py:11
  55.5 12.6 %collective-permute-start.4 = (f32[16,1024]{1,0:T(8,128)}, f32[16,1024]{1,0:T(8,128)S(1)}, u32[]{:S(2)}, u32[]{:S(2)}) collective-permute-start(f32[16,1024]{1,0:T(8,128)} %shard_map.113), channel_id=1, source_target_pairs={{0,16},{4,20},{8,24},{12,28},{16,32},{20,36},{24,40},{28,44},{32,4... | collective-permute-start | bytes 196616 | tf_op jit(solution)/shard_map/ppermute | solution.py:11
  68.2 10.8 %collective-permute-start.5 = (f32[16,1024]{1,0:T(8,128)S(1)}, f32[16,1024]{1,0:T(8,128)S(1)}, u32[]{:S(2)}, u32[]{:S(2)}) collective-permute-start(f32[16,1024]{1,0:T(8,128)S(1)} %multiply_add_fusion.2), channel_id=1, source_target_pairs={{0,16},{4,20},{8,24},{12,28},{16,32},{20,36},{24,40},{28,44},{32,4... | collective-permute-start | bytes 196616 | tf_op jit(solution)/shard_map/ppermute | solution.py:11
  70.1 14.0 %collective-permute-start.6 = (f32[16,1024]{1,0:T(8,128)S(1)}, f32[16,1024]{1,0:T(8,128)S(1)}, u32[]{:S(2)}, u32[]{:S(2)}) collective-permute-start(f32[16,1024]{1,0:T(8,128)S(1)} %multiply_add_fusion.2), channel_id=1, source_target_pairs={{0,32},{4,36},{8,40},{12,44},{16,48},{20,52},{24,56},{28,60},{32,6... | collective-permute-start | bytes 196616 | tf_op jit(solution)/shard_map/ppermute | solution.py:11
  72.5 13.2 %collective-permute-start.7 = (f32[16,1024]{1,0:T(8,128)S(1)}, f32[16,1024]{1,0:T(8,128)S(1)}, u32[]{:S(2)}, u32[]{:S(2)}) collective-permute-start(f32[16,1024]{1,0:T(8,128)S(1)} %multiply_add_fusion.2), channel_id=1, source_target_pairs={{0,48},{4,52},{8,56},{12,60},{16,64},{20,68},{24,72},{28,76},{32,8... | collective-permute-start | bytes 196616 | tf_op jit(solution)/shard_map/ppermute | solution.py:11
  85.7 5.0 %collective-permute-start.10 = (f32[16,1024]{1,0:T(8,128)S(1)}, f32[16,1024]{1,0:T(8,128)S(1)}, u32[]{:S(2)}, u32[]{:S(2)}) collective-permute-start(f32[16,1024]{1,0:T(8,128)S(1)} %multiply_add_fusion.1), channel_id=1, source_target_pairs={{0,192},{4,196},{8,200},{12,204},{16,208},{20,212},{24,216},{28,22... | collective-permute-start | bytes 196616 | tf_op jit(solution)/shard_map/ppermute | solution.py:11
  86.4 13.2 %collective-permute-start.8 = (f32[16,1024]{1,0:T(8,128)S(1)}, f32[16,1024]{1,0:T(8,128)S(1)}, u32[]{:S(2)}, u32[]{:S(2)}) collective-permute-start(f32[16,1024]{1,0:T(8,128)S(1)} %multiply_add_fusion.1), channel_id=1, source_target_pairs={{0,64},{4,68},{8,72},{12,76},{16,80},{20,84},{24,88},{28,92},{32,9... | collective-permute-start | bytes 196616 | tf_op jit(solution)/shard_map/ppermute | solution.py:11
  88.3 11.2 %collective-permute-start.9 = (f32[16,1024]{1,0:T(8,128)S(1)}, f32[16,1024]{1,0:T(8,128)S(1)}, u32[]{:S(2)}, u32[]{:S(2)}) collective-permute-start(f32[16,1024]{1,0:T(8,128)S(1)} %multiply_add_fusion.1), channel_id=1, source_target_pairs={{0,128},{4,132},{8,136},{12,140},{16,144},{20,148},{24,152},{28,15... | collective-permute-start | bytes 196616 | tf_op jit(solution)/shard_map/ppermute | solution.py:11
  89.6 9.9 %copy-start.8 = (f32[16,1024]{1,0:T(8,128)S(1)}, f32[16,1024]{1,0:T(8,128)}, u32[]{:S(2)}) copy-start(f32[16,1024]{1,0:T(8,128)} %param.19) | copy-start | bytes 196612

commit v2 on v1

--- a/solution.py
+++ b/solution.py
@@ -3,10 +3,18 @@
 from jax import lax
 from jax.experimental import pallas as pl
 from jax.experimental.pallas import tpu as pltpu
-from jax.sharding import PartitionSpec as P
+from jax.sharding import Mesh, PartitionSpec as P
+
+CTX = ("xh", "z", "y")
+LINK = jnp.float32
+
+
+def ctx_size():
+    return lax.axis_size("xh") * lax.axis_size("z") * lax.axis_size("y")
+
 
 def shifted(shard, axis, by):
-    devices = lax.axis_size(axis)
+    devices = ctx_size() if axis == CTX else lax.axis_size(axis)
     pairs = [(i, i + by) for i in range(devices) if 0 <= i + by < devices]
     return lax.ppermute(shard, axis, pairs)
 
@@ -42,22 +50,31 @@
     return res * jnp.sqrt(-jnp.expm1(-2.0 * rate))
 
 
+def prefix(gathered, decay, me):
+    before = jnp.zeros_like(gathered[0])
+    total = jnp.zeros_like(gathered[0])
+    for e in range(gathered.shape[0]):
+        total = total * decay + gathered[e]
+        before = jnp.where(e < me, total, before)
+    return before, total
+
+
 def carry_in(ends, rate, width):
-    devices = lax.axis_size("ctx")
-    radix = 4
-    state = shifted(ends, "ctx", 1)
-    for j in range(2, radix + 1):
-        if j < devices:
-            state = state + jnp.exp(-width * (j - 1) * rate) * shifted(ends, "ctx", j)
-    span = radix
-    while span < devices:
-        total = state
-        for j in range(1, radix):
-            if j * span < devices:
-                total = total + jnp.exp(-width * (j * span) * rate) * shifted(state, "ctx", j * span)
-        state = total
-        span *= radix
-    return state
+    ny, nz = lax.axis_size("y"), lax.axis_size("z")
+    y, z, x = lax.axis_index("y"), lax.axis_index("z"), lax.axis_index("xh")
+    channels = ends.shape[1]
+    quarter = channels // ny
+    own = lax.dynamic_slice_in_dim(rate, y * quarter, quarter, 1)
+    first = lax.all_gather(ends.astype(LINK), "y").astype(jnp.float32)
+    in_group, group_end = prefix(first, jnp.exp(-width * rate), y)
+    part = lax.dynamic_slice_in_dim(group_end, y * quarter, quarter, 1)
+    second = lax.all_gather(part.astype(LINK), "z").astype(jnp.float32)
+    in_half, half_end = prefix(second, jnp.exp(-width * ny * own), z)
+    third = lax.all_gather(half_end.astype(LINK), "xh").astype(jnp.float32)
+    in_whole, _ = prefix(third, jnp.exp(-width * ny * nz * own), x)
+    group_start = in_half + jnp.exp(-width * ny * z.astype(jnp.float32) * own) * in_whole
+    group_start = lax.all_gather(group_start.astype(LINK), "y", axis=1, tiled=True).astype(jnp.float32)
+    return in_group + jnp.exp(-width * y.astype(jnp.float32) * rate) * group_start
 
 
 LANES = 512
@@ -155,7 +172,7 @@
     ]
     small_rows = sum(r.shape[0] for r in rims)
     fill = jnp.zeros((-(-small_rows // pack) * pack - small_rows, q_mr.shape[1]), q_mr.dtype)
-    got = shifted(jnp.concatenate([u_tail, jnp.concatenate(rims + [fill])]), "ctx", 1)
+    got = shifted(jnp.concatenate([u_tail, jnp.concatenate(rims + [fill])]), CTX, 1)
     u_rim = got[sent_rows - u_rows : sent_rows]
     at = sent_rows
     q_rim = got[at : at + q_rows]
@@ -190,17 +207,22 @@
 
 
 def solution(mesh):
+    ctx, mp = mesh.shape["ctx"], mesh.shape["mp"]
+    ny = 4
+    nz = 8
+    nx = ctx // (ny * nz)
+    grid = Mesh(mesh.devices.reshape(nx, nz, ny, mp), ("xh", "z", "y", "mp"))
     in_specs = (
-        P("ctx", "mp"),
-        P("ctx", "mp"),
-        P("ctx", "mp"),
-        P("ctx", "mp"),
-        P("ctx", "mp"),
+        P(CTX, "mp"),
+        P(CTX, "mp"),
+        P(CTX, "mp"),
+        P(CTX, "mp"),
+        P(CTX, "mp"),
         P(None, None, "mp"),
         P(None, "mp"),
         P("mp"),
         P(None, "mp"),
         P(None, "mp"),
     )
-    out_specs = (P("ctx", "mp"), P("ctx", "mp"))
-    return jax.shard_map(shards, mesh=mesh, in_specs=in_specs, out_specs=out_specs, check_vma=False)
+    out_specs = (P(CTX, "mp"), P(CTX, "mp"))
+    return jax.shard_map(shards, mesh=grid, in_specs=in_specs, out_specs=out_specs, check_vma=False)

time: 110 us -> 119 us (1.082)
  blocking collectives: 5.77 us -> 60.8 us
  waiting for transfers between devices: 40.2 us -> 14.6 us
  starting transfers between devices: 24 us -> 3.47 us
    all_gather x0 -> x4, blocking collectives: none -> 55.1 us  [the longest x1 24.6 us: carry_in(): second = lax.all_gather(part.astype(LINK), 'z').astype(jnp.float32)]
    ppermute x11 -> x1, waiting for transfers between devices: 40.2 us -> 14.6 us  [shifted(): return lax.ppermute(shard, axis, pairs)]
    ppermute x11 -> x1, starting transfers between devices: 24 us -> 3.47 us  [shifted(): return lax.ppermute(shard, axis, pairs)]
    concatenate x1, local copies, waits for them, and re-layouts: 0.18 us -> 2.61 us  [shards(): jnp.concatenate([u_tail, jnp.concatenate(rims + [fill])])]
    rev x1, local copies, waits for them, and re-layouts: 2.62 us -> 0.24 us  [long_conv(): kernel = taps[::-1][:, None, :]]
  transfers between devices with their start and end apart: 11 -> 1, of which waited for: 9 -> 1; matrix products, arithmetic and copies ran while one was open for 4% -> 1% of each run, Pallas kernels for 0% -> 0%
where the time goes in v2:
time: 119 us; the launch traced here: 118 us
  blocking collectives  60.8 us (51%)
  waiting for transfers between devices  14.6 us (12%)
  matrix products  11 us (9%)
  Pallas kernels  9.99 us (8%)
  other arithmetic  9.54 us (8%)
  local copies, waits for them, and re-layouts  8.05 us (7%)
  starting transfers between devices  3.47 us (3%)
    all_gather x1, blocking collectives, carry_in(): second = lax.all_gather(part.astype(LINK), 'z').astype(jnp.float32)  24.6 us
    ppermute x1, waiting for transfers between devices, shifted(): return lax.ppermute(shard, axis, pairs)  14.6 us
    all_gather x1, blocking collectives, carry_in(): first = lax.all_gather(ends.astype(LINK), 'y').astype(jnp.float32)  12.7 us
    all_gather x1, blocking collectives, carry_in(): lax.all_gather(group_start.astype(LINK), 'y', axis=1, tiled=True)  11.9 us
    conv_general_dilated x1, matrix products, long_conv(): lax.conv_general_dilated(extended[None], kernel, (1,), 'VALID', dimension...  11 us
    pallas_call x1, Pallas kernels, recur_output(): pl.pallas_call(_output_kernel, out_shape=jax.ShapeDtypeStruct(u.shape, jn...  6.8 us
    all_gather x1, blocking collectives, carry_in(): third = lax.all_gather(half_end.astype(LINK), 'xh').astype(jnp.float32)  5.91 us
    psum x1, blocking collectives, shards(): totals = lax.psum(jnp.sum(mixer_ext * mixer_ext, axis=1), 'mp')  5.77 us
  transfers between devices with their start and end apart: 1, of which 1 were waited for; matrix products, arithmetic and copies ran while one was open for 1% of the time, Pallas kernels for 0%

profile of v2, /device:TPU:6, one launch (start us, length us, event | category | flops | bytes accessed | tf_op | source)
XLA Modules:
  0.0 118.5 jit_solution(15484584525578552237)
XLA Ops:
  0.6 0.0 copy-start.1
  0.6 0.0 copy-start.8
  0.7 0.0 copy-start.3
  0.7 0.0 copy-start.4
  0.7 0.8 slice.277
  1.5 1.2 %slice_convert_fusion.1 = (f32[146,1024]{1,0:T(8,128)S(1)}, f32[146,1024]{1,0:T(8,128)S(1)}) fusion(bf16[256,1024]{1,0:T(8,128)(2,1)} %param.12, bf16[256,1024]{1,0:T(8,128)(2,1)} %param.11), kind=kLoop, calls=%fused_computation.62 | loop fusion | flops 299008 | bytes 1794048 | tf_op jit(solution)/shard_map/convert_element_type | solution.py:28
  2.8 0.0 copy-done.1
  2.8 0.0 copy-done.8
  2.8 0.1 fusion.34
  2.9 0.0 copy-done.3
  2.9 0.7 slice.279
  3.6 0.0 copy-done.4
  3.6 0.0 copy-start.6
  3.6 0.4 fusion.24
  4.0 0.0 copy-start.2
  4.0 0.0 copy-start
  4.1 2.6 %concatenate.21 = bf16[160,1024]{1,0:T(8,128)(2,1)} concatenate(bf16[144,1024]{1,0:T(8,128)(2,1)S(1)} %fusion.24, bf16[4,1024]{1,0:T(4,128)(2,1)S(1)} %slice.276, bf16[2,1024]{1,0:T(2,128)(2,1)S(1)} %slice.277, bf16[2,1024]{1,0:T(2,128)(2,1)S(1)} %slice.278, bf16[2,1024]{1,0:T(2,128)(2,1)S(1)} %slice.279, bf16[2,1024]{1,0:T(2,128)(2,1)S(1)} %slice.280, ...), dimensions={0} | concatenate | bytes 655360 | tf_op jit(solution)/shard_map/concatenate | solution.py:175
  6.7 3.5 %collective-permute-start = (bf16[160,1024]{1,0:T(8,128)(2,1)}, bf16[160,1024]{1,0:T(8,128)(2,1)}, u32[]{:S(2)}, u32[]{:S(2)}) collective-permute-start(bf16[160,1024]{1,0:T(8,128)(2,1)} %concatenate.21), channel_id=1, source_target_pairs={{0,4},{4,8},{8,12},{12,16},{16,20},{20,24},{24,28},{28,32},{32,36}... | collective-permute-start | bytes 983048 | tf_op jit(solution)/shard_map/ppermute | solution.py:19
  10.2 0.0 copy-done.6
  10.2 0.2 rev.3
  10.5 0.0 copy-done.2
  10.5 0.6 negate_exponential_fusion.a_ref
  11.1 14.6 %collective-permute-done = bf16[160,1024]{1,0:T(8,128)(2,1)} collective-permute-done((bf16[160,1024]{1,0:T(8,128)(2,1)}, bf16[160,1024]{1,0:T(8,128)(2,1)}, u32[]{:S(2)}, u32[]{:S(2)}) %collective-permute-start) | collective-permute-done | bytes 327712 | tf_op jit(solution)/shard_map/ppermute | solution.py:19
  25.7 0.8 fusion.33
  26.6 0.0 copy-done
  26.6 0.1 maximum_convert_fusion.1
  26.7 0.1 maximum_convert_fusion.2
  26.9 0.7 slice.351
  27.6 0.1 maximum_convert_fusion
  27.7 0.7 fusion.18
  28.4 1.0 slice.355
  29.5 0.1 maximum_bitcast_fusion
  29.6 11.0 %fusion = f32[1,258,1024]{2,0,1:T(1,128)S(1)} fusion(bf16[1,385,1024]{2,1,0:T(8,128)(2,1)S(1)} %maximum_bitcast_fusion, f32[128,1,1024]{2,0,1:T(8,128)S(1)} %bitcast.24), kind=kOutput, calls=%fused_computation | convolution fusion | flops 405798912 | bytes 2369536 | tf_op jit(solution)/shard_map/conv_general_dilated | solution.py:38
  40.6 0.7 multiply_reduce_fusion
  41.2 5.8 %psum.7 = f32[258]{0:T(512)S(1)} all-reduce(f32[258]{0:T(512)S(1)} %get-tuple-element.4), channel_id=1, replica_groups=mesh['xh'=2,'z'=8,'y'=4,'mp'=4] {'mp'}, use_global_device_ids=true, to_apply=%region_1.0 | all-reduce | flops 258 | bytes 2064 | tf_op jit(solution)/shard_map/psum | solution.py:198
  47.0 0.1 maximum_convert_fusion.4
  47.2 0.9 slice.577
  48.1 0.2 multiply_reduce-precision_fusion
  48.3 1.7 %fusion.8.u_ref = f32[256,1024]{1,0:T(8,128)} fusion(f32[258,1024]{1,0:T(8,128)S(1)} %multiply_reduce-precision_fusion, f32[258,1024]{1,0:T(8,128)S(1)} %maximum_convert_fusion.4, f32[1024]{0:T(1024)S(1)} %bitcast.41, f32[1024]{0:T(1024)S(1)} %bitcast.42, f32[1024]{0:T(1024)S(1)} %bitcast.37, f32[1024]{0:T(1024)S(1)} %bitcast.38, f32[1024]{0:T(1024)S(1)} %bitcast.39, ...), kind=kLoop, calls=%fused_computation.14 | loop fusion | flops 3145728 | bytes 7364608 | tf_op jit(solution)/shard_map/reduce_precision | solution.py:23
  50.0 3.2 %shard_map.113 = f32[16,1024]{1,0:T(8,128)} custom-call(f32[256,1024]{1,0:T(8,128)} %fusion.8.u_ref, f32[16,1024]{1,0:T(8,128)} %negate_exponential_fusion.a_ref), custom_call_target="tpu_custom_call" | custom-call | flops 8388608 | bytes 1179648 | tf_op jit(solution)/shard_map/pallas_call | solution.py:119
  53.2 12.7 %all-gather = f32[64,1024]{1,0:T(8,128)S(1)} all-gather(f32[16,1024]{1,0:T(8,128)} %shard_map.113), channel_id=2, replica_groups=mesh['xh'=2,'z'=8,'y'=4,'mp'=4] {'y'}, dimensions={0}, use_global_device_ids=true | all-gather | bytes 327680 | tf_op jit(solution)/shard_map/all_gather | solution.py:68
  65.9 24.6 %all-gather.1 = f32[128,256]{1,0:T(8,128)S(1)} all-gather(f32[16,256]{1,0:T(8,128)S(1)} %constant_dynamic-slice_fusion), channel_id=3, replica_groups=mesh['xh'=2,'z'=8,'y'=4,'mp'=4] {'z'}, dimensions={0}, use_global_device_ids=true | all-gather | bytes 147456 | tf_op jit(solution)/shard_map/all_gather | solution.py:71
  90.5 5.9 %all-gather.2 = f32[32,256]{1,0:T(8,128)S(1)} all-gather(f32[16,256]{1,0:T(8,128)S(1)} %get-tuple-element.2), channel_id=4, replica_groups=mesh['xh'=2,'z'=8,'y'=4,'mp'=4] {'xh'}, dimensions={0}, use_global_device_ids=true | all-gather | bytes 49152 | tf_op jit(solution)/shard_map/all_gather | solution.py:73
  96.5 11.9 %all_gather.27 = f32[16,1024]{1,0:T(8,128)S(1)} all-gather(f32[16,256]{1,0:T(8,128)S(1)} %fusion.31), channel_id=1, replica_groups=mesh['xh'=2,'z'=8,'y'=4,'mp'=4] {'y'}, dimensions={1}, use_global_device_ids=true | all-gather | bytes 81920 | tf_op jit(solution)/shard_map/all_gather | solution.py:76
  108.4 0.1 maximum_convert_fusion.3
  108.5 0.7 multiply_add_fusion
  109.3 6.8 %shard_map.114 = f32[256,1024]{1,0:T(8,128)} custom-call(f32[256,1024]{1,0:T(8,128)} %fusion.8.u_ref, f32[16,1024]{1,0:T(8,128)} %negate_exponential_fusion.a_ref, f32[16,1024]{1,0:T(8,128)} %get-tuple-element.29.w_ref, f32[16,1024]{1,0:T(8,128)} %get-tuple-element.28.s0_ref), custom_call_target="tpu_custom_call" | custom-call | flops 16777216 | bytes 2293760 | tf_op jit(solution)/shard_map/pallas_call | solution.py:133
  116.1 2.4 %fusion.14 = bf16[256,1024]{1,0:T(8,128)(2,1)} fusion(f32[258,1024]{1,0:T(8,128)S(1)} %maximum_convert_fusion.3, f32[256,1024]{1,0:T(8,128)} %shard_map.114, f32[1024]{0:T(1024)S(1)} %bitcast.44, f32[1024]{0:T(1024)S(1)} %bitcast.45, f32[1024]{0:T(1024)S(1)} %bitcast.43), kind=kLoop, calls=%fused_computation.26 | loop fusion | flops 2097152 | bytes 4730880 | tf_op jit(solution)/shard_map/convert_element_type | solution.py:205
  (15 shorter events, 0.2 us)
Async XLA Ops:
  0.6 2.1 %copy-start.1 = (bf16[256,1024]{1,0:T(8,128)(2,1)S(1)}, bf16[256,1024]{1,0:T(8,128)(2,1)}, u32[]{:S(2)}) copy-start(bf16[256,1024]{1,0:T(8,128)(2,1)} %param.12) | copy-start | bytes 1572868
  0.6 2.1 %copy-start.8 = (f32[6,3,1024]{2,1,0:T(4,128)S(1)}, f32[6,3,1024]{2,1,0:T(4,128)}, u32[]{:S(2)}) copy-start(f32[6,3,1024]{2,1,0:T(4,128)} %param.15) | copy-start | bytes 221188
  0.7 2.2 %copy-start.3 = (bf16[256,1024]{1,0:T(8,128)(2,1)S(1)}, bf16[256,1024]{1,0:T(8,128)(2,1)}, u32[]{:S(2)}) copy-start(bf16[256,1024]{1,0:T(8,128)(2,1)} %param.10) | copy-start | bytes 1572868
  0.7 2.9 %copy-start.4 = (bf16[256,1024]{1,0:T(8,128)(2,1)S(1)}, bf16[256,1024]{1,0:T(8,128)(2,1)}, u32[]{:S(2)}) copy-start(bf16[256,1024]{1,0:T(8,128)(2,1)} %param.14) | copy-start | bytes 1572868
  3.6 6.6 %copy-start.6 = (f32[128,1024]{1,0:T(8,128)S(1)}, f32[128,1024]{1,0:T(8,128)}, u32[]{:S(2)}) copy-start(f32[128,1024]{1,0:T(8,128)} %param.16) | copy-start | bytes 1572868
  4.0 6.4 %copy-start.2 = (f32[16,1024]{1,0:T(8,128)S(1)}, f32[16,1024]{1,0:T(8,128)}, u32[]{:S(2)}) copy-start(f32[16,1024]{1,0:T(8,128)} %param.18) | copy-start | bytes 196612
  4.0 22.5 %copy-start = (bf16[256,1024]{1,0:T(8,128)(2,1)S(1)}, bf16[256,1024]{1,0:T(8,128)(2,1)}, u32[]{:S(2)}) copy-start(bf16[256,1024]{1,0:T(8,128)(2,1)} %param.11) | copy-start | bytes 1572868
  6.7 19.1 %collective-permute-start = (bf16[160,1024]{1,0:T(8,128)(2,1)}, bf16[160,1024]{1,0:T(8,128)(2,1)}, u32[]{:S(2)}, u32[]{:S(2)}) collective-permute-start(bf16[160,1024]{1,0:T(8,128)(2,1)} %concatenate.21), channel_id=1, source_target_pairs={{0,4},{4,8},{8,12},{12,16},{16,20},{20,24},{24,28},{28,32},{32,36}... | collective-permute-start | bytes 983048 | tf_op jit(solution)/shard_map/ppermute | solution.py:19
  47.0 1.1 copy-start.9
  50.0 58.4 %copy-start.5 = (bf16[256,1024]{1,0:T(8,128)(2,1)S(1)}, bf16[256,1024]{1,0:T(8,128)(2,1)}, u32[]{:S(2)}) copy-start(bf16[256,1024]{1,0:T(8,128)(2,1)} %param.13) | copy-start | bytes 1572868
  90.5 18.0 %copy-start.7 = (f32[16,1024]{1,0:T(8,128)S(1)}, f32[16,1024]{1,0:T(8,128)}, u32[]{:S(2)}) copy-start(f32[16,1024]{1,0:T(8,128)} %param.19) | copy-start | bytes 196612

commit v3 on v1

--- a/solution.py
+++ b/solution.py
@@ -45,16 +45,19 @@
 def carry_in(ends, rate, width):
     devices = lax.axis_size("ctx")
     radix = 4
-    state = shifted(ends, "ctx", 1)
+    sent = ends.astype(jnp.bfloat16)
+    state = shifted(sent, "ctx", 1).astype(jnp.float32)
     for j in range(2, radix + 1):
         if j < devices:
-            state = state + jnp.exp(-width * (j - 1) * rate) * shifted(ends, "ctx", j)
+            state = state + jnp.exp(-width * (j - 1) * rate) * shifted(sent, "ctx", j).astype(jnp.float32)
     span = radix
     while span < devices:
         total = state
+        sent = state.astype(jnp.bfloat16)
         for j in range(1, radix):
             if j * span < devices:
-                total = total + jnp.exp(-width * (j * span) * rate) * shifted(state, "ctx", j * span)
+                got = shifted(sent, "ctx", j * span).astype(jnp.float32)
+                total = total + jnp.exp(-width * (j * span) * rate) * got
         state = total
         span *= radix
     return state

time: 110 us -> 108 us (0.982)
  waiting for transfers between devices: 40.2 us -> 37.1 us
    ppermute x11, waiting for transfers between devices: 40.2 us -> 37.1 us  [shifted(): return lax.ppermute(shard, axis, pairs)]
where the time goes in v3:
time: 108 us; the launch traced here: 107 us
  waiting for transfers between devices  37.1 us (34%)
  starting transfers between devices  24 us (22%)
  matrix products  11 us (10%)
  other arithmetic  10.5 us (10%)
  Pallas kernels  9.96 us (9%)
  local copies, waits for them, and re-layouts  8.06 us (7%)
  blocking collectives  5.77 us (5%)
    ppermute x11, waiting for transfers between devices, shifted(): return lax.ppermute(shard, axis, pairs)  37.1 us
    ppermute x11, starting transfers between devices, shifted(): return lax.ppermute(shard, axis, pairs)  24 us
    conv_general_dilated x1, matrix products, long_conv(): lax.conv_general_dilated(extended[None], kernel, (1,), 'VALID', dimension...  11 us
    pallas_call x1, Pallas kernels, recur_output(): pl.pallas_call(_output_kernel, out_shape=jax.ShapeDtypeStruct(u.shape, jn...  6.77 us
    psum x1, blocking collectives, shards(): totals = lax.psum(jnp.sum(mixer_ext * mixer_ext, axis=1), 'mp')  5.77 us
    pallas_call x1, Pallas kernels, recur_ends(): pl.pallas_call(_ends_kernel, out_shape=jax.ShapeDtypeStruct(a.shape, jnp....  3.19 us
    rev x1, local copies, waits for them, and re-layouts, long_conv(): kernel = taps[::-1][:, None, :]  2.62 us
    convert_element_type x1, other arithmetic, shards(): mixer_li = (lq * long_li).astype(jnp.bfloat16)  2.41 us
  transfers between devices with their start and end apart: 11, of which 9 were waited for; matrix products, arithmetic and copies ran while one was open for 4% of the time, Pallas kernels for 0%

profile of v3, /device:TPU:6, one launch (start us, length us, event | category | flops | bytes accessed | tf_op | source)
XLA Modules:
  0.0 107.3 jit_solution(16659988931875491924)
XLA Ops:
  0.7 0.8 slice.235
  1.5 1.2 %slice_convert_fusion.1 = (f32[146,1024]{1,0:T(8,128)S(1)}, f32[146,1024]{1,0:T(8,128)S(1)}) fusion(bf16[256,1024]{1,0:T(8,128)(2,1)} %param.12, bf16[256,1024]{1,0:T(8,128)(2,1)} %param.11), kind=kLoop, calls=%fused_computation.62 | loop fusion | flops 299008 | bytes 1794048 | tf_op jit(solution)/shard_map/convert_element_type | solution.py:20
  2.9 0.7 slice.237
  3.6 0.4 fusion.24
  4.1 0.2 concatenate.21
  4.2 3.5 %collective-permute-start = (bf16[160,1024]{1,0:T(8,128)(2,1)S(1)}, bf16[160,1024]{1,0:T(8,128)(2,1)}, u32[]{:S(2)}, u32[]{:S(2)}) collective-permute-start(bf16[160,1024]{1,0:T(8,128)(2,1)S(1)} %concatenate.21), channel_id=1, source_target_pairs={{0,4},{4,8},{8,12},{12,16},{16,20},{20,24},{24,28},{28,32},{32,36}... | collective-permute-start | bytes 983048 | tf_op jit(solution)/shard_map/ppermute | solution.py:11
  7.7 2.6 %rev.3 = f32[128,1024]{1,0:T(8,128)} reverse(f32[128,1024]{1,0:T(8,128)S(1)} %copy-done.6), dimensions={0} | reverse | bytes 1048576 | tf_op jit(solution)/shard_map/rev | solution.py:29
  10.4 0.6 negate_exponential_fusion.a_ref
  11.0 12.1 %collective-permute-done = bf16[160,1024]{1,0:T(8,128)(2,1)} collective-permute-done((bf16[160,1024]{1,0:T(8,128)(2,1)S(1)}, bf16[160,1024]{1,0:T(8,128)(2,1)}, u32[]{:S(2)}, u32[]{:S(2)}) %collective-permute-start) | collective-permute-done | bytes 327712 | tf_op jit(solution)/shard_map/ppermute | solution.py:11
  23.1 0.8 fusion.32
  23.9 0.1 maximum_convert_fusion.1
  24.1 0.1 maximum_convert_fusion.2
  24.2 0.7 slice.281
  25.0 0.1 maximum_convert_fusion
  25.1 0.7 fusion.18
  25.8 1.1 %slice.285 = bf16[129,1024]{1,0:T(8,128)(2,1)S(1)} slice(bf16[160,1024]{1,0:T(8,128)(2,1)} %collective-permute-done), slice={[15:144], [0:1024]} | slice | bytes 528384 | tf_op jit(solution)/shard_map/slice | solution.py:162
  26.9 0.1 maximum_bitcast_fusion
  27.1 11.0 %fusion = f32[1,258,1024]{2,0,1:T(1,128)S(1)} fusion(bf16[1,385,1024]{2,1,0:T(8,128)(2,1)S(1)} %maximum_bitcast_fusion, f32[128,1,1024]{2,0,1:T(8,128)S(1)} %bitcast.24), kind=kOutput, calls=%fused_computation | convolution fusion | flops 405798912 | bytes 2369536 | tf_op jit(solution)/shard_map/conv_general_dilated | solution.py:30
  38.0 0.7 multiply_reduce_fusion
  38.7 5.8 %psum.7 = f32[258]{0:T(512)S(1)} all-reduce(f32[258]{0:T(512)S(1)} %get-tuple-element.4), channel_id=1, replica_groups=mesh['ctx'=64,'mp'=4] {'mp'}, use_global_device_ids=true, to_apply=%region_1.0 | all-reduce | flops 258 | bytes 2064 | tf_op jit(solution)/shard_map/psum | solution.py:184
  44.5 0.1 maximum_convert_fusion.4
  44.7 0.2 multiply_reduce-precision_fusion
  44.9 1.7 %fusion.8.u_ref = f32[256,1024]{1,0:T(8,128)} fusion(f32[258,1024]{1,0:T(8,128)S(1)} %multiply_reduce-precision_fusion, f32[258,1024]{1,0:T(8,128)S(1)} %maximum_convert_fusion.4, f32[1024]{0:T(1024)S(1)} %bitcast.41, f32[1024]{0:T(1024)S(1)} %bitcast.42, f32[1024]{0:T(1024)S(1)} %bitcast.37, f32[1024]{0:T(1024)S(1)} %bitcast.38, f32[1024]{0:T(1024)S(1)} %bitcast.39, ...), kind=kLoop, calls=%fused_computation.14 | loop fusion | flops 3145728 | bytes 7364608 | tf_op jit(solution)/shard_map/reduce_precision | solution.py:15
  46.5 3.2 %shard_map.113 = f32[16,1024]{1,0:T(8,128)} custom-call(f32[256,1024]{1,0:T(8,128)} %fusion.8.u_ref, f32[16,1024]{1,0:T(8,128)} %negate_exponential_fusion.a_ref), custom_call_target="tpu_custom_call" | custom-call | flops 8388608 | bytes 1179648 | tf_op jit(solution)/shard_map/pallas_call | solution.py:105
  49.7 0.8 convert_element_type.80
  50.6 1.9 %collective-permute-start.1 = (bf16[16,1024]{1,0:T(8,128)(2,1)S(1)}, bf16[16,1024]{1,0:T(8,128)(2,1)S(1)}, u32[]{:S(2)}, u32[]{:S(2)}) collective-permute-start(bf16[16,1024]{1,0:T(8,128)(2,1)S(1)} %convert_element_type.80), channel_id=1, source_target_pairs={{0,4},{4,8},{8,12},{12,16},{16,20},{20,24},{24,28},{28,32},{32,36}... | collective-permute-start | bytes 98312 | tf_op jit(solution)/shard_map/ppermute | solution.py:11
  52.5 1.9 %collective-permute-start.2 = (bf16[16,1024]{1,0:T(8,128)(2,1)S(1)}, bf16[16,1024]{1,0:T(8,128)(2,1)S(1)}, u32[]{:S(2)}, u32[]{:S(2)}) collective-permute-start(bf16[16,1024]{1,0:T(8,128)(2,1)S(1)} %convert_element_type.80), channel_id=1, source_target_pairs={{0,8},{4,12},{8,16},{12,20},{16,24},{20,28},{24,32},{28,36},{32,40... | collective-permute-start | bytes 98312 | tf_op jit(solution)/shard_map/ppermute | solution.py:11
  54.4 1.9 %collective-permute-start.3 = (bf16[16,1024]{1,0:T(8,128)(2,1)S(1)}, bf16[16,1024]{1,0:T(8,128)(2,1)S(1)}, u32[]{:S(2)}, u32[]{:S(2)}) collective-permute-start(bf16[16,1024]{1,0:T(8,128)(2,1)S(1)} %convert_element_type.80), channel_id=1, source_target_pairs={{0,12},{4,16},{8,20},{12,24},{16,28},{20,32},{24,36},{28,40},{32,4... | collective-permute-start | bytes 98312 | tf_op jit(solution)/shard_map/ppermute | solution.py:11
  56.4 3.5 %collective-permute-start.4 = (bf16[16,1024]{1,0:T(8,128)(2,1)S(1)}, bf16[16,1024]{1,0:T(8,128)(2,1)S(1)}, u32[]{:S(2)}, u32[]{:S(2)}) collective-permute-start(bf16[16,1024]{1,0:T(8,128)(2,1)S(1)} %convert_element_type.80), channel_id=1, source_target_pairs={{0,16},{4,20},{8,24},{12,28},{16,32},{20,36},{24,40},{28,44},{32,4... | collective-permute-start | bytes 98312 | tf_op jit(solution)/shard_map/ppermute | solution.py:11
  59.8 2.3 %collective-permute-done.1 = bf16[16,1024]{1,0:T(8,128)(2,1)S(1)} collective-permute-done((bf16[16,1024]{1,0:T(8,128)(2,1)S(1)}, bf16[16,1024]{1,0:T(8,128)(2,1)S(1)}, u32[]{:S(2)}, u32[]{:S(2)}) %collective-permute-start.1) | collective-permute-done | bytes 32800 | tf_op jit(solution)/shard_map/ppermute | solution.py:11
  62.1 2.2 %collective-permute-done.2 = bf16[16,1024]{1,0:T(8,128)(2,1)S(1)} collective-permute-done((bf16[16,1024]{1,0:T(8,128)(2,1)S(1)}, bf16[16,1024]{1,0:T(8,128)(2,1)S(1)}, u32[]{:S(2)}, u32[]{:S(2)}) %collective-permute-start.2) | collective-permute-done | bytes 32800 | tf_op jit(solution)/shard_map/ppermute | solution.py:11
  64.3 2.5 %collective-permute-done.3 = bf16[16,1024]{1,0:T(8,128)(2,1)S(1)} collective-permute-done((bf16[16,1024]{1,0:T(8,128)(2,1)S(1)}, bf16[16,1024]{1,0:T(8,128)(2,1)S(1)}, u32[]{:S(2)}, u32[]{:S(2)}) %collective-permute-start.3) | collective-permute-done | bytes 32800 | tf_op jit(solution)/shard_map/ppermute | solution.py:11
  66.8 1.6 %collective-permute-done.4 = bf16[16,1024]{1,0:T(8,128)(2,1)S(1)} collective-permute-done((bf16[16,1024]{1,0:T(8,128)(2,1)S(1)}, bf16[16,1024]{1,0:T(8,128)(2,1)S(1)}, u32[]{:S(2)}, u32[]{:S(2)}) %collective-permute-start.4) | collective-permute-done | bytes 32800 | tf_op jit(solution)/shard_map/ppermute | solution.py:11
  68.5 1.9 %collective-permute-start.5 = (bf16[16,1024]{1,0:T(8,128)(2,1)S(1)}, bf16[16,1024]{1,0:T(8,128)(2,1)S(1)}, u32[]{:S(2)}, u32[]{:S(2)}) collective-permute-start(bf16[16,1024]{1,0:T(8,128)(2,1)S(1)} %fusion.29), channel_id=1, source_target_pairs={{0,16},{4,20},{8,24},{12,28},{16,32},{20,36},{24,40},{28,44},{32,4... | collective-permute-start | bytes 98312 | tf_op jit(solution)/shard_map/ppermute | solution.py:11
  70.4 2.4 %collective-permute-start.6 = (bf16[16,1024]{1,0:T(8,128)(2,1)S(1)}, bf16[16,1024]{1,0:T(8,128)(2,1)S(1)}, u32[]{:S(2)}, u32[]{:S(2)}) collective-permute-start(bf16[16,1024]{1,0:T(8,128)(2,1)S(1)} %fusion.29), channel_id=1, source_target_pairs={{0,32},{4,36},{8,40},{12,44},{16,48},{20,52},{24,56},{28,60},{32,6... | collective-permute-start | bytes 98312 | tf_op jit(solution)/shard_map/ppermute | solution.py:11
  72.8 3.1 %collective-permute-start.7 = (bf16[16,1024]{1,0:T(8,128)(2,1)S(1)}, bf16[16,1024]{1,0:T(8,128)(2,1)S(1)}, u32[]{:S(2)}, u32[]{:S(2)}) collective-permute-start(bf16[16,1024]{1,0:T(8,128)(2,1)S(1)} %fusion.29), channel_id=1, source_target_pairs={{0,48},{4,52},{8,56},{12,60},{16,64},{20,68},{24,72},{28,76},{32,8... | collective-permute-start | bytes 98312 | tf_op jit(solution)/shard_map/ppermute | solution.py:11
  75.9 2.0 %collective-permute-done.5 = bf16[16,1024]{1,0:T(8,128)(2,1)S(1)} collective-permute-done((bf16[16,1024]{1,0:T(8,128)(2,1)S(1)}, bf16[16,1024]{1,0:T(8,128)(2,1)S(1)}, u32[]{:S(2)}, u32[]{:S(2)}) %collective-permute-start.5) | collective-permute-done | bytes 32800 | tf_op jit(solution)/shard_map/ppermute | solution.py:11
  77.9 3.2 %collective-permute-done.6 = bf16[16,1024]{1,0:T(8,128)(2,1)S(1)} collective-permute-done((bf16[16,1024]{1,0:T(8,128)(2,1)S(1)}, bf16[16,1024]{1,0:T(8,128)(2,1)S(1)}, u32[]{:S(2)}, u32[]{:S(2)}) %collective-permute-start.6) | collective-permute-done | bytes 32800 | tf_op jit(solution)/shard_map/ppermute | solution.py:11
  81.1 3.4 %collective-permute-done.7 = bf16[16,1024]{1,0:T(8,128)(2,1)S(1)} collective-permute-done((bf16[16,1024]{1,0:T(8,128)(2,1)S(1)}, bf16[16,1024]{1,0:T(8,128)(2,1)S(1)}, u32[]{:S(2)}, u32[]{:S(2)}) %collective-permute-start.7) | collective-permute-done | bytes 32800 | tf_op jit(solution)/shard_map/ppermute | solution.py:11
  84.6 0.7 collective-permute-start.10
  85.2 1.9 %collective-permute-start.8 = (bf16[16,1024]{1,0:T(8,128)(2,1)S(1)}, bf16[16,1024]{1,0:T(8,128)(2,1)S(1)}, u32[]{:S(2)}, u32[]{:S(2)}) collective-permute-start(bf16[16,1024]{1,0:T(8,128)(2,1)S(1)} %get-tuple-element.2), channel_id=1, source_target_pairs={{0,64},{4,68},{8,72},{12,76},{16,80},{20,84},{24,88},{28,92},{32,9... | collective-permute-start | bytes 98312 | tf_op jit(solution)/shard_map/ppermute | solution.py:11
  87.2 1.3 %collective-permute-start.9 = (bf16[16,1024]{1,0:T(8,128)(2,1)S(1)}, bf16[16,1024]{1,0:T(8,128)(2,1)S(1)}, u32[]{:S(2)}, u32[]{:S(2)}) collective-permute-start(bf16[16,1024]{1,0:T(8,128)(2,1)S(1)} %get-tuple-element.2), channel_id=1, source_target_pairs={{0,128},{4,132},{8,136},{12,140},{16,144},{20,148},{24,152},{28,15... | collective-permute-start | bytes 98312 | tf_op jit(solution)/shard_map/ppermute | solution.py:11
  88.5 0.1 maximum_convert_fusion.3
  88.6 0.9 slice.423
  89.6 7.8 %collective-permute-done.8 = bf16[16,1024]{1,0:T(8,128)(2,1)S(1)} collective-permute-done((bf16[16,1024]{1,0:T(8,128)(2,1)S(1)}, bf16[16,1024]{1,0:T(8,128)(2,1)S(1)}, u32[]{:S(2)}, u32[]{:S(2)}) %collective-permute-start.8) | collective-permute-done | bytes 32800 | tf_op jit(solution)/shard_map/ppermute | solution.py:11
  97.4 0.7 multiply_add_fusion
  98.1 6.8 %shard_map.114 = f32[256,1024]{1,0:T(8,128)} custom-call(f32[256,1024]{1,0:T(8,128)} %fusion.8.u_ref, f32[16,1024]{1,0:T(8,128)} %negate_exponential_fusion.a_ref, f32[16,1024]{1,0:T(8,128)} %get-tuple-element.29.w_ref, f32[16,1024]{1,0:T(8,128)} %get-tuple-element.28.s0_ref), custom_call_target="tpu_custom_call" | custom-call | flops 16777216 | bytes 2293760 | tf_op jit(solution)/shard_map/pallas_call | solution.py:119
  104.9 2.4 %fusion.14 = bf16[256,1024]{1,0:T(8,128)(2,1)} fusion(f32[258,1024]{1,0:T(8,128)S(1)} %maximum_convert_fusion.3, f32[256,1024]{1,0:T(8,128)} %shard_map.114, f32[1024]{0:T(1024)S(1)} %bitcast.44, f32[1024]{0:T(1024)S(1)} %bitcast.45, f32[1024]{0:T(1024)S(1)} %bitcast.43), kind=kLoop, calls=%fused_computation.26 | loop fusion | flops 2097152 | bytes 4730880 | tf_op jit(solution)/shard_map/convert_element_type | solution.py:191
  (32 shorter events, 0.3 us)
Async XLA Ops:
  0.6 2.1 %copy-start.1 = (bf16[256,1024]{1,0:T(8,128)(2,1)S(1)}, bf16[256,1024]{1,0:T(8,128)(2,1)}, u32[]{:S(2)}) copy-start(bf16[256,1024]{1,0:T(8,128)(2,1)} %param.12) | copy-start | bytes 1572868
  0.6 2.1 %copy-start.9 = (f32[6,3,1024]{2,1,0:T(4,128)S(1)}, f32[6,3,1024]{2,1,0:T(4,128)}, u32[]{:S(2)}) copy-start(f32[6,3,1024]{2,1,0:T(4,128)} %param.15) | copy-start | bytes 221188
  0.7 2.2 %copy-start.3 = (bf16[256,1024]{1,0:T(8,128)(2,1)S(1)}, bf16[256,1024]{1,0:T(8,128)(2,1)}, u32[]{:S(2)}) copy-start(bf16[256,1024]{1,0:T(8,128)(2,1)} %param.10) | copy-start | bytes 1572868
  0.7 2.9 %copy-start.4 = (bf16[256,1024]{1,0:T(8,128)(2,1)S(1)}, bf16[256,1024]{1,0:T(8,128)(2,1)}, u32[]{:S(2)}) copy-start(bf16[256,1024]{1,0:T(8,128)(2,1)} %param.14) | copy-start | bytes 1572868
  3.6 4.1 %copy-start.6 = (f32[128,1024]{1,0:T(8,128)S(1)}, f32[128,1024]{1,0:T(8,128)}, u32[]{:S(2)}) copy-start(f32[128,1024]{1,0:T(8,128)} %param.16) | copy-start | bytes 1572868
  4.0 6.3 %copy-start.2 = (f32[16,1024]{1,0:T(8,128)S(1)}, f32[16,1024]{1,0:T(8,128)}, u32[]{:S(2)}) copy-start(f32[16,1024]{1,0:T(8,128)} %param.18) | copy-start | bytes 196612
  4.0 19.9 %copy-start = (bf16[256,1024]{1,0:T(8,128)(2,1)S(1)}, bf16[256,1024]{1,0:T(8,128)(2,1)}, u32[]{:S(2)}) copy-start(bf16[256,1024]{1,0:T(8,128)(2,1)} %param.11) | copy-start | bytes 1572868
  4.2 18.9 %collective-permute-start = (bf16[160,1024]{1,0:T(8,128)(2,1)S(1)}, bf16[160,1024]{1,0:T(8,128)(2,1)}, u32[]{:S(2)}, u32[]{:S(2)}) collective-permute-start(bf16[160,1024]{1,0:T(8,128)(2,1)S(1)} %concatenate.21), channel_id=1, source_target_pairs={{0,4},{4,8},{8,12},{12,16},{16,20},{20,24},{24,28},{28,32},{32,36}... | collective-permute-start | bytes 983048 | tf_op jit(solution)/shard_map/ppermute | solution.py:11
  25.8 1.3 %copy-start.7 = (f32[128,1024]{1,0:T(8,128)S(1)}, f32[128,1024]{1,0:T(8,128)}, u32[]{:S(2)}) copy-start(f32[128,1024]{1,0:T(8,128)} %rev.3) | copy-start | bytes 1572868
  38.7 5.9 %copy-start.10 = (f32[1024]{0:T(1024)S(1)}, f32[1024]{0:T(1024)}, u32[]{:S(2)}) copy-start(f32[1024]{0:T(1024)} %param.17) | copy-start | bytes 12292
  46.5 41.9 %copy-start.5 = (bf16[256,1024]{1,0:T(8,128)(2,1)S(1)}, bf16[256,1024]{1,0:T(8,128)(2,1)}, u32[]{:S(2)}) copy-start(bf16[256,1024]{1,0:T(8,128)(2,1)} %param.13) | copy-start | bytes 1572868
  50.6 11.5 %collective-permute-start.1 = (bf16[16,1024]{1,0:T(8,128)(2,1)S(1)}, bf16[16,1024]{1,0:T(8,128)(2,1)S(1)}, u32[]{:S(2)}, u32[]{:S(2)}) collective-permute-start(bf16[16,1024]{1,0:T(8,128)(2,1)S(1)} %convert_element_type.80), channel_id=1, source_target_pairs={{0,4},{4,8},{8,12},{12,16},{16,20},{20,24},{24,28},{28,32},{32,36}... | collective-permute-start | bytes 98312 | tf_op jit(solution)/shard_map/ppermute | solution.py:11
  52.5 11.8 %collective-permute-start.2 = (bf16[16,1024]{1,0:T(8,128)(2,1)S(1)}, bf16[16,1024]{1,0:T(8,128)(2,1)S(1)}, u32[]{:S(2)}, u32[]{:S(2)}) collective-permute-start(bf16[16,1024]{1,0:T(8,128)(2,1)S(1)} %convert_element_type.80), channel_id=1, source_target_pairs={{0,8},{4,12},{8,16},{12,20},{16,24},{20,28},{24,32},{28,36},{32,40... | collective-permute-start | bytes 98312 | tf_op jit(solution)/shard_map/ppermute | solution.py:11
  54.4 12.4 %collective-permute-start.3 = (bf16[16,1024]{1,0:T(8,128)(2,1)S(1)}, bf16[16,1024]{1,0:T(8,128)(2,1)S(1)}, u32[]{:S(2)}, u32[]{:S(2)}) collective-permute-start(bf16[16,1024]{1,0:T(8,128)(2,1)S(1)} %convert_element_type.80), channel_id=1, source_target_pairs={{0,12},{4,16},{8,20},{12,24},{16,28},{20,32},{24,36},{28,40},{32,4... | collective-permute-start | bytes 98312 | tf_op jit(solution)/shard_map/ppermute | solution.py:11
  56.4 12.1 %collective-permute-start.4 = (bf16[16,1024]{1,0:T(8,128)(2,1)S(1)}, bf16[16,1024]{1,0:T(8,128)(2,1)S(1)}, u32[]{:S(2)}, u32[]{:S(2)}) collective-permute-start(bf16[16,1024]{1,0:T(8,128)(2,1)S(1)} %convert_element_type.80), channel_id=1, source_target_pairs={{0,16},{4,20},{8,24},{12,28},{16,32},{20,36},{24,40},{28,44},{32,4... | collective-permute-start | bytes 98312 | tf_op jit(solution)/shard_map/ppermute | solution.py:11
  68.5 9.4 %collective-permute-start.5 = (bf16[16,1024]{1,0:T(8,128)(2,1)S(1)}, bf16[16,1024]{1,0:T(8,128)(2,1)S(1)}, u32[]{:S(2)}, u32[]{:S(2)}) collective-permute-start(bf16[16,1024]{1,0:T(8,128)(2,1)S(1)} %fusion.29), channel_id=1, source_target_pairs={{0,16},{4,20},{8,24},{12,28},{16,32},{20,36},{24,40},{28,44},{32,4... | collective-permute-start | bytes 98312 | tf_op jit(solution)/shard_map/ppermute | solution.py:11
  70.4 10.7 %collective-permute-start.6 = (bf16[16,1024]{1,0:T(8,128)(2,1)S(1)}, bf16[16,1024]{1,0:T(8,128)(2,1)S(1)}, u32[]{:S(2)}, u32[]{:S(2)}) collective-permute-start(bf16[16,1024]{1,0:T(8,128)(2,1)S(1)} %fusion.29), channel_id=1, source_target_pairs={{0,32},{4,36},{8,40},{12,44},{16,48},{20,52},{24,56},{28,60},{32,6... | collective-permute-start | bytes 98312 | tf_op jit(solution)/shard_map/ppermute | solution.py:11
  72.8 11.6 %collective-permute-start.7 = (bf16[16,1024]{1,0:T(8,128)(2,1)S(1)}, bf16[16,1024]{1,0:T(8,128)(2,1)S(1)}, u32[]{:S(2)}, u32[]{:S(2)}) collective-permute-start(bf16[16,1024]{1,0:T(8,128)(2,1)S(1)} %fusion.29), channel_id=1, source_target_pairs={{0,48},{4,52},{8,56},{12,60},{16,64},{20,68},{24,72},{28,76},{32,8... | collective-permute-start | bytes 98312 | tf_op jit(solution)/shard_map/ppermute | solution.py:11
  84.6 5.0 %collective-permute-start.10 = (bf16[16,1024]{1,0:T(8,128)(2,1)S(1)}, bf16[16,1024]{1,0:T(8,128)(2,1)S(1)}, u32[]{:S(2)}, u32[]{:S(2)}) collective-permute-start(bf16[16,1024]{1,0:T(8,128)(2,1)S(1)} %get-tuple-element.2), channel_id=1, source_target_pairs={{0,192},{4,196},{8,200},{12,204},{16,208},{20,212},{24,216},{28,22... | collective-permute-start | bytes 98312 | tf_op jit(solution)/shard_map/ppermute | solution.py:11
  85.2 12.1 %collective-permute-start.8 = (bf16[16,1024]{1,0:T(8,128)(2,1)S(1)}, bf16[16,1024]{1,0:T(8,128)(2,1)S(1)}, u32[]{:S(2)}, u32[]{:S(2)}) collective-permute-start(bf16[16,1024]{1,0:T(8,128)(2,1)S(1)} %get-tuple-element.2), channel_id=1, source_target_pairs={{0,64},{4,68},{8,72},{12,76},{16,80},{20,84},{24,88},{28,92},{32,9... | collective-permute-start | bytes 98312 | tf_op jit(solution)/shard_map/ppermute | solution.py:11
  87.2 10.2 %collective-permute-start.9 = (bf16[16,1024]{1,0:T(8,128)(2,1)S(1)}, bf16[16,1024]{1,0:T(8,128)(2,1)S(1)}, u32[]{:S(2)}, u32[]{:S(2)}) collective-permute-start(bf16[16,1024]{1,0:T(8,128)(2,1)S(1)} %get-tuple-element.2), channel_id=1, source_target_pairs={{0,128},{4,132},{8,136},{12,140},{16,144},{20,148},{24,152},{28,15... | collective-permute-start | bytes 98312 | tf_op jit(solution)/shard_map/ppermute | solution.py:11
  88.5 8.9 %copy-start.8 = (f32[16,1024]{1,0:T(8,128)S(1)}, f32[16,1024]{1,0:T(8,128)}, u32[]{:S(2)}) copy-start(f32[16,1024]{1,0:T(8,128)} %param.19) | copy-start | bytes 196612

commit v4 on v3

--- a/solution.py
+++ b/solution.py
@@ -63,7 +63,7 @@
     return state
 
 
-LANES = 512
+LANES = 1024
 
 
 def _recur_body(u_ref, a_ref, w_ref, s0_ref, y_ref, end_ref):

time: 108 us -> 108 us (level)
  no operation moved by 1% of the time
where the time goes in v4:
time: 108 us
  waiting for transfers between devices  37.1 us (34%)
  starting transfers between devices  24 us (22%)
  matrix products  11 us (10%)
  other arithmetic  10.5 us (10%)
  Pallas kernels  10.3 us (10%)
  local copies, waits for them, and re-layouts  8.06 us (7%)
  blocking collectives  5.77 us (5%)
    ppermute x11, waiting for transfers between devices, shifted(): return lax.ppermute(shard, axis, pairs)  37.1 us
    ppermute x11, starting transfers between devices, shifted(): return lax.ppermute(shard, axis, pairs)  24 us
    conv_general_dilated x1, matrix products, long_conv(): lax.conv_general_dilated(extended[None], kernel, (1,), 'VALID', dimension...  11 us
    pallas_call x1, Pallas kernels, recur_output(): pl.pallas_call(_output_kernel, out_shape=jax.ShapeDtypeStruct(u.shape, jn...  6.86 us
    psum x1, blocking collectives, shards(): totals = lax.psum(jnp.sum(mixer_ext * mixer_ext, axis=1), 'mp')  5.77 us
    pallas_call x1, Pallas kernels, recur_ends(): pl.pallas_call(_ends_kernel, out_shape=jax.ShapeDtypeStruct(a.shape, jnp....  3.46 us
    rev x1, local copies, waits for them, and re-layouts, long_conv(): kernel = taps[::-1][:, None, :]  2.62 us
    convert_element_type x1, other arithmetic, shards(): mixer_li = (lq * long_li).astype(jnp.bfloat16)  2.41 us
  transfers between devices with their start and end apart: 11, of which 9 were waited for; matrix products, arithmetic and copies ran while one was open for 4% of the time, Pallas kernels for 0%

profile of v4, /device:TPU:6, one launch (start us, length us, event | category | flops | bytes accessed | tf_op | source)
XLA Modules:
  0.0 107.6 jit_solution(2887480397042801324)
XLA Ops:
  0.7 0.8 slice.235
  1.5 1.2 %slice_convert_fusion.1 = (f32[146,1024]{1,0:T(8,128)S(1)}, f32[146,1024]{1,0:T(8,128)S(1)}) fusion(bf16[256,1024]{1,0:T(8,128)(2,1)} %param.12, bf16[256,1024]{1,0:T(8,128)(2,1)} %param.11), kind=kLoop, calls=%fused_computation.62 | loop fusion | flops 299008 | bytes 1794048 | tf_op jit(solution)/shard_map/convert_element_type | solution.py:20
  2.9 0.7 slice.237
  3.6 0.4 fusion.24
  4.1 0.2 concatenate.21
  4.2 3.5 %collective-permute-start = (bf16[160,1024]{1,0:T(8,128)(2,1)S(1)}, bf16[160,1024]{1,0:T(8,128)(2,1)}, u32[]{:S(2)}, u32[]{:S(2)}) collective-permute-start(bf16[160,1024]{1,0:T(8,128)(2,1)S(1)} %concatenate.21), channel_id=1, source_target_pairs={{0,4},{4,8},{8,12},{12,16},{16,20},{20,24},{24,28},{28,32},{32,36}... | collective-permute-start | bytes 983048 | tf_op jit(solution)/shard_map/ppermute | solution.py:11
  7.7 2.6 %rev.3 = f32[128,1024]{1,0:T(8,128)} reverse(f32[128,1024]{1,0:T(8,128)S(1)} %copy-done.6), dimensions={0} | reverse | bytes 1048576 | tf_op jit(solution)/shard_map/rev | solution.py:29
  10.4 0.6 negate_exponential_fusion.a_ref
  11.0 12.1 %collective-permute-done = bf16[160,1024]{1,0:T(8,128)(2,1)} collective-permute-done((bf16[160,1024]{1,0:T(8,128)(2,1)S(1)}, bf16[160,1024]{1,0:T(8,128)(2,1)}, u32[]{:S(2)}, u32[]{:S(2)}) %collective-permute-start) | collective-permute-done | bytes 327712 | tf_op jit(solution)/shard_map/ppermute | solution.py:11
  23.1 0.8 fusion.32
  23.9 0.1 maximum_convert_fusion.1
  24.1 0.1 maximum_convert_fusion.2
  24.2 0.7 slice.281
  25.0 0.1 maximum_convert_fusion
  25.1 0.7 fusion.18
  25.8 1.1 %slice.285 = bf16[129,1024]{1,0:T(8,128)(2,1)S(1)} slice(bf16[160,1024]{1,0:T(8,128)(2,1)} %collective-permute-done), slice={[15:144], [0:1024]} | slice | bytes 528384 | tf_op jit(solution)/shard_map/slice | solution.py:162
  26.9 0.1 maximum_bitcast_fusion
  27.1 11.0 %fusion = f32[1,258,1024]{2,0,1:T(1,128)S(1)} fusion(bf16[1,385,1024]{2,1,0:T(8,128)(2,1)S(1)} %maximum_bitcast_fusion, f32[128,1,1024]{2,0,1:T(8,128)S(1)} %bitcast.24), kind=kOutput, calls=%fused_computation | convolution fusion | flops 405798912 | bytes 2369536 | tf_op jit(solution)/shard_map/conv_general_dilated | solution.py:30
  38.0 0.7 multiply_reduce_fusion
  38.7 5.8 %psum.7 = f32[258]{0:T(512)S(1)} all-reduce(f32[258]{0:T(512)S(1)} %get-tuple-element.4), channel_id=1, replica_groups=mesh['ctx'=64,'mp'=4] {'mp'}, use_global_device_ids=true, to_apply=%region_1.0 | all-reduce | flops 258 | bytes 2064 | tf_op jit(solution)/shard_map/psum | solution.py:184
  44.5 0.1 maximum_convert_fusion.4
  44.7 0.2 multiply_reduce-precision_fusion
  44.9 1.7 %fusion.8.u_ref = f32[256,1024]{1,0:T(8,128)} fusion(f32[258,1024]{1,0:T(8,128)S(1)} %multiply_reduce-precision_fusion, f32[258,1024]{1,0:T(8,128)S(1)} %maximum_convert_fusion.4, f32[1024]{0:T(1024)S(1)} %bitcast.41, f32[1024]{0:T(1024)S(1)} %bitcast.42, f32[1024]{0:T(1024)S(1)} %bitcast.37, f32[1024]{0:T(1024)S(1)} %bitcast.38, f32[1024]{0:T(1024)S(1)} %bitcast.39, ...), kind=kLoop, calls=%fused_computation.14 | loop fusion | flops 3145728 | bytes 7364608 | tf_op jit(solution)/shard_map/reduce_precision | solution.py:15
  46.5 3.5 %shard_map.113 = f32[16,1024]{1,0:T(8,128)} custom-call(f32[256,1024]{1,0:T(8,128)} %fusion.8.u_ref, f32[16,1024]{1,0:T(8,128)} %negate_exponential_fusion.a_ref), custom_call_target="tpu_custom_call" | custom-call | flops 8388608 | bytes 1179648 | tf_op jit(solution)/shard_map/pallas_call | solution.py:105
  50.0 0.8 convert_element_type.80
  50.9 1.9 %collective-permute-start.1 = (bf16[16,1024]{1,0:T(8,128)(2,1)S(1)}, bf16[16,1024]{1,0:T(8,128)(2,1)S(1)}, u32[]{:S(2)}, u32[]{:S(2)}) collective-permute-start(bf16[16,1024]{1,0:T(8,128)(2,1)S(1)} %convert_element_type.80), channel_id=1, source_target_pairs={{0,4},{4,8},{8,12},{12,16},{16,20},{20,24},{24,28},{28,32},{32,36}... | collective-permute-start | bytes 98312 | tf_op jit(solution)/shard_map/ppermute | solution.py:11
  52.8 1.9 %collective-permute-start.2 = (bf16[16,1024]{1,0:T(8,128)(2,1)S(1)}, bf16[16,1024]{1,0:T(8,128)(2,1)S(1)}, u32[]{:S(2)}, u32[]{:S(2)}) collective-permute-start(bf16[16,1024]{1,0:T(8,128)(2,1)S(1)} %convert_element_type.80), channel_id=1, source_target_pairs={{0,8},{4,12},{8,16},{12,20},{16,24},{20,28},{24,32},{28,36},{32,40... | collective-permute-start | bytes 98312 | tf_op jit(solution)/shard_map/ppermute | solution.py:11
  54.7 1.9 %collective-permute-start.3 = (bf16[16,1024]{1,0:T(8,128)(2,1)S(1)}, bf16[16,1024]{1,0:T(8,128)(2,1)S(1)}, u32[]{:S(2)}, u32[]{:S(2)}) collective-permute-start(bf16[16,1024]{1,0:T(8,128)(2,1)S(1)} %convert_element_type.80), channel_id=1, source_target_pairs={{0,12},{4,16},{8,20},{12,24},{16,28},{20,32},{24,36},{28,40},{32,4... | collective-permute-start | bytes 98312 | tf_op jit(solution)/shard_map/ppermute | solution.py:11
  56.6 3.5 %collective-permute-start.4 = (bf16[16,1024]{1,0:T(8,128)(2,1)S(1)}, bf16[16,1024]{1,0:T(8,128)(2,1)S(1)}, u32[]{:S(2)}, u32[]{:S(2)}) collective-permute-start(bf16[16,1024]{1,0:T(8,128)(2,1)S(1)} %convert_element_type.80), channel_id=1, source_target_pairs={{0,16},{4,20},{8,24},{12,28},{16,32},{20,36},{24,40},{28,44},{32,4... | collective-permute-start | bytes 98312 | tf_op jit(solution)/shard_map/ppermute | solution.py:11
  60.1 2.3 %collective-permute-done.1 = bf16[16,1024]{1,0:T(8,128)(2,1)S(1)} collective-permute-done((bf16[16,1024]{1,0:T(8,128)(2,1)S(1)}, bf16[16,1024]{1,0:T(8,128)(2,1)S(1)}, u32[]{:S(2)}, u32[]{:S(2)}) %collective-permute-start.1) | collective-permute-done | bytes 32800 | tf_op jit(solution)/shard_map/ppermute | solution.py:11
  62.4 2.2 %collective-permute-done.2 = bf16[16,1024]{1,0:T(8,128)(2,1)S(1)} collective-permute-done((bf16[16,1024]{1,0:T(8,128)(2,1)S(1)}, bf16[16,1024]{1,0:T(8,128)(2,1)S(1)}, u32[]{:S(2)}, u32[]{:S(2)}) %collective-permute-start.2) | collective-permute-done | bytes 32800 | tf_op jit(solution)/shard_map/ppermute | solution.py:11
  64.6 2.5 %collective-permute-done.3 = bf16[16,1024]{1,0:T(8,128)(2,1)S(1)} collective-permute-done((bf16[16,1024]{1,0:T(8,128)(2,1)S(1)}, bf16[16,1024]{1,0:T(8,128)(2,1)S(1)}, u32[]{:S(2)}, u32[]{:S(2)}) %collective-permute-start.3) | collective-permute-done | bytes 32800 | tf_op jit(solution)/shard_map/ppermute | solution.py:11
  67.1 1.6 %collective-permute-done.4 = bf16[16,1024]{1,0:T(8,128)(2,1)S(1)} collective-permute-done((bf16[16,1024]{1,0:T(8,128)(2,1)S(1)}, bf16[16,1024]{1,0:T(8,128)(2,1)S(1)}, u32[]{:S(2)}, u32[]{:S(2)}) %collective-permute-start.4) | collective-permute-done | bytes 32800 | tf_op jit(solution)/shard_map/ppermute | solution.py:11
  68.8 1.9 %collective-permute-start.5 = (bf16[16,1024]{1,0:T(8,128)(2,1)S(1)}, bf16[16,1024]{1,0:T(8,128)(2,1)S(1)}, u32[]{:S(2)}, u32[]{:S(2)}) collective-permute-start(bf16[16,1024]{1,0:T(8,128)(2,1)S(1)} %fusion.29), channel_id=1, source_target_pairs={{0,16},{4,20},{8,24},{12,28},{16,32},{20,36},{24,40},{28,44},{32,4... | collective-permute-start | bytes 98312 | tf_op jit(solution)/shard_map/ppermute | solution.py:11
  70.7 2.4 %collective-permute-start.6 = (bf16[16,1024]{1,0:T(8,128)(2,1)S(1)}, bf16[16,1024]{1,0:T(8,128)(2,1)S(1)}, u32[]{:S(2)}, u32[]{:S(2)}) collective-permute-start(bf16[16,1024]{1,0:T(8,128)(2,1)S(1)} %fusion.29), channel_id=1, source_target_pairs={{0,32},{4,36},{8,40},{12,44},{16,48},{20,52},{24,56},{28,60},{32,6... | collective-permute-start | bytes 98312 | tf_op jit(solution)/shard_map/ppermute | solution.py:11
  73.1 3.1 %collective-permute-start.7 = (bf16[16,1024]{1,0:T(8,128)(2,1)S(1)}, bf16[16,1024]{1,0:T(8,128)(2,1)S(1)}, u32[]{:S(2)}, u32[]{:S(2)}) collective-permute-start(bf16[16,1024]{1,0:T(8,128)(2,1)S(1)} %fusion.29), channel_id=1, source_target_pairs={{0,48},{4,52},{8,56},{12,60},{16,64},{20,68},{24,72},{28,76},{32,8... | collective-permute-start | bytes 98312 | tf_op jit(solution)/shard_map/ppermute | solution.py:11
  76.2 2.0 %collective-permute-done.5 = bf16[16,1024]{1,0:T(8,128)(2,1)S(1)} collective-permute-done((bf16[16,1024]{1,0:T(8,128)(2,1)S(1)}, bf16[16,1024]{1,0:T(8,128)(2,1)S(1)}, u32[]{:S(2)}, u32[]{:S(2)}) %collective-permute-start.5) | collective-permute-done | bytes 32800 | tf_op jit(solution)/shard_map/ppermute | solution.py:11
  78.2 3.2 %collective-permute-done.6 = bf16[16,1024]{1,0:T(8,128)(2,1)S(1)} collective-permute-done((bf16[16,1024]{1,0:T(8,128)(2,1)S(1)}, bf16[16,1024]{1,0:T(8,128)(2,1)S(1)}, u32[]{:S(2)}, u32[]{:S(2)}) %collective-permute-start.6) | collective-permute-done | bytes 32800 | tf_op jit(solution)/shard_map/ppermute | solution.py:11
  81.4 3.4 %collective-permute-done.7 = bf16[16,1024]{1,0:T(8,128)(2,1)S(1)} collective-permute-done((bf16[16,1024]{1,0:T(8,128)(2,1)S(1)}, bf16[16,1024]{1,0:T(8,128)(2,1)S(1)}, u32[]{:S(2)}, u32[]{:S(2)}) %collective-permute-start.7) | collective-permute-done | bytes 32800 | tf_op jit(solution)/shard_map/ppermute | solution.py:11
  84.8 0.7 collective-permute-start.10
  85.5 1.9 %collective-permute-start.8 = (bf16[16,1024]{1,0:T(8,128)(2,1)S(1)}, bf16[16,1024]{1,0:T(8,128)(2,1)S(1)}, u32[]{:S(2)}, u32[]{:S(2)}) collective-permute-start(bf16[16,1024]{1,0:T(8,128)(2,1)S(1)} %get-tuple-element.2), channel_id=1, source_target_pairs={{0,64},{4,68},{8,72},{12,76},{16,80},{20,84},{24,88},{28,92},{32,9... | collective-permute-start | bytes 98312 | tf_op jit(solution)/shard_map/ppermute | solution.py:11
  87.4 1.3 %collective-permute-start.9 = (bf16[16,1024]{1,0:T(8,128)(2,1)S(1)}, bf16[16,1024]{1,0:T(8,128)(2,1)S(1)}, u32[]{:S(2)}, u32[]{:S(2)}) collective-permute-start(bf16[16,1024]{1,0:T(8,128)(2,1)S(1)} %get-tuple-element.2), channel_id=1, source_target_pairs={{0,128},{4,132},{8,136},{12,140},{16,144},{20,148},{24,152},{28,15... | collective-permute-start | bytes 98312 | tf_op jit(solution)/shard_map/ppermute | solution.py:11
  88.8 0.1 maximum_convert_fusion.3
  88.9 0.9 slice.423
  89.8 7.8 %collective-permute-done.8 = bf16[16,1024]{1,0:T(8,128)(2,1)S(1)} collective-permute-done((bf16[16,1024]{1,0:T(8,128)(2,1)S(1)}, bf16[16,1024]{1,0:T(8,128)(2,1)S(1)}, u32[]{:S(2)}, u32[]{:S(2)}) %collective-permute-start.8) | collective-permute-done | bytes 32800 | tf_op jit(solution)/shard_map/ppermute | solution.py:11
  97.6 0.7 multiply_add_fusion
  98.4 6.9 %shard_map.114 = f32[256,1024]{1,0:T(8,128)} custom-call(f32[256,1024]{1,0:T(8,128)} %fusion.8.u_ref, f32[16,1024]{1,0:T(8,128)} %negate_exponential_fusion.a_ref, f32[16,1024]{1,0:T(8,128)} %get-tuple-element.29.w_ref, f32[16,1024]{1,0:T(8,128)} %get-tuple-element.28.s0_ref), custom_call_target="tpu_custom_call" | custom-call | flops 16777216 | bytes 2293760 | tf_op jit(solution)/shard_map/pallas_call | solution.py:119
  105.2 2.4 %fusion.14 = bf16[256,1024]{1,0:T(8,128)(2,1)} fusion(f32[258,1024]{1,0:T(8,128)S(1)} %maximum_convert_fusion.3, f32[256,1024]{1,0:T(8,128)} %shard_map.114, f32[1024]{0:T(1024)S(1)} %bitcast.44, f32[1024]{0:T(1024)S(1)} %bitcast.45, f32[1024]{0:T(1024)S(1)} %bitcast.43), kind=kLoop, calls=%fused_computation.26 | loop fusion | flops 2097152 | bytes 4730880 | tf_op jit(solution)/shard_map/convert_element_type | solution.py:191
  (32 shorter events, 0.3 us)
Async XLA Ops:
  0.6 2.1 %copy-start.1 = (bf16[256,1024]{1,0:T(8,128)(2,1)S(1)}, bf16[256,1024]{1,0:T(8,128)(2,1)}, u32[]{:S(2)}) copy-start(bf16[256,1024]{1,0:T(8,128)(2,1)} %param.12) | copy-start | bytes 1572868
  0.6 2.1 %copy-start.9 = (f32[6,3,1024]{2,1,0:T(4,128)S(1)}, f32[6,3,1024]{2,1,0:T(4,128)}, u32[]{:S(2)}) copy-start(f32[6,3,1024]{2,1,0:T(4,128)} %param.15) | copy-start | bytes 221188
  0.7 2.2 %copy-start.3 = (bf16[256,1024]{1,0:T(8,128)(2,1)S(1)}, bf16[256,1024]{1,0:T(8,128)(2,1)}, u32[]{:S(2)}) copy-start(bf16[256,1024]{1,0:T(8,128)(2,1)} %param.10) | copy-start | bytes 1572868
  0.7 2.9 %copy-start.4 = (bf16[256,1024]{1,0:T(8,128)(2,1)S(1)}, bf16[256,1024]{1,0:T(8,128)(2,1)}, u32[]{:S(2)}) copy-start(bf16[256,1024]{1,0:T(8,128)(2,1)} %param.14) | copy-start | bytes 1572868
  3.6 4.1 %copy-start.6 = (f32[128,1024]{1,0:T(8,128)S(1)}, f32[128,1024]{1,0:T(8,128)}, u32[]{:S(2)}) copy-start(f32[128,1024]{1,0:T(8,128)} %param.16) | copy-start | bytes 1572868
  4.0 6.3 %copy-start.2 = (f32[16,1024]{1,0:T(8,128)S(1)}, f32[16,1024]{1,0:T(8,128)}, u32[]{:S(2)}) copy-start(f32[16,1024]{1,0:T(8,128)} %param.18) | copy-start | bytes 196612
  4.0 19.9 %copy-start = (bf16[256,1024]{1,0:T(8,128)(2,1)S(1)}, bf16[256,1024]{1,0:T(8,128)(2,1)}, u32[]{:S(2)}) copy-start(bf16[256,1024]{1,0:T(8,128)(2,1)} %param.11) | copy-start | bytes 1572868
  4.2 18.9 %collective-permute-start = (bf16[160,1024]{1,0:T(8,128)(2,1)S(1)}, bf16[160,1024]{1,0:T(8,128)(2,1)}, u32[]{:S(2)}, u32[]{:S(2)}) collective-permute-start(bf16[160,1024]{1,0:T(8,128)(2,1)S(1)} %concatenate.21), channel_id=1, source_target_pairs={{0,4},{4,8},{8,12},{12,16},{16,20},{20,24},{24,28},{28,32},{32,36}... | collective-permute-start | bytes 983048 | tf_op jit(solution)/shard_map/ppermute | solution.py:11
  25.8 1.3 %copy-start.7 = (f32[128,1024]{1,0:T(8,128)S(1)}, f32[128,1024]{1,0:T(8,128)}, u32[]{:S(2)}) copy-start(f32[128,1024]{1,0:T(8,128)} %rev.3) | copy-start | bytes 1572868
  38.7 5.9 %copy-start.10 = (f32[1024]{0:T(1024)S(1)}, f32[1024]{0:T(1024)}, u32[]{:S(2)}) copy-start(f32[1024]{0:T(1024)} %param.17) | copy-start | bytes 12292
  46.5 42.2 %copy-start.5 = (bf16[256,1024]{1,0:T(8,128)(2,1)S(1)}, bf16[256,1024]{1,0:T(8,128)(2,1)}, u32[]{:S(2)}) copy-start(bf16[256,1024]{1,0:T(8,128)(2,1)} %param.13) | copy-start | bytes 1572868
  50.9 11.5 %collective-permute-start.1 = (bf16[16,1024]{1,0:T(8,128)(2,1)S(1)}, bf16[16,1024]{1,0:T(8,128)(2,1)S(1)}, u32[]{:S(2)}, u32[]{:S(2)}) collective-permute-start(bf16[16,1024]{1,0:T(8,128)(2,1)S(1)} %convert_element_type.80), channel_id=1, source_target_pairs={{0,4},{4,8},{8,12},{12,16},{16,20},{20,24},{24,28},{28,32},{32,36}... | collective-permute-start | bytes 98312 | tf_op jit(solution)/shard_map/ppermute | solution.py:11
  52.8 11.8 %collective-permute-start.2 = (bf16[16,1024]{1,0:T(8,128)(2,1)S(1)}, bf16[16,1024]{1,0:T(8,128)(2,1)S(1)}, u32[]{:S(2)}, u32[]{:S(2)}) collective-permute-start(bf16[16,1024]{1,0:T(8,128)(2,1)S(1)} %convert_element_type.80), channel_id=1, source_target_pairs={{0,8},{4,12},{8,16},{12,20},{16,24},{20,28},{24,32},{28,36},{32,40... | collective-permute-start | bytes 98312 | tf_op jit(solution)/shard_map/ppermute | solution.py:11
  54.7 12.4 %collective-permute-start.3 = (bf16[16,1024]{1,0:T(8,128)(2,1)S(1)}, bf16[16,1024]{1,0:T(8,128)(2,1)S(1)}, u32[]{:S(2)}, u32[]{:S(2)}) collective-permute-start(bf16[16,1024]{1,0:T(8,128)(2,1)S(1)} %convert_element_type.80), channel_id=1, source_target_pairs={{0,12},{4,16},{8,20},{12,24},{16,28},{20,32},{24,36},{28,40},{32,4... | collective-permute-start | bytes 98312 | tf_op jit(solution)/shard_map/ppermute | solution.py:11
  56.6 12.1 %collective-permute-start.4 = (bf16[16,1024]{1,0:T(8,128)(2,1)S(1)}, bf16[16,1024]{1,0:T(8,128)(2,1)S(1)}, u32[]{:S(2)}, u32[]{:S(2)}) collective-permute-start(bf16[16,1024]{1,0:T(8,128)(2,1)S(1)} %convert_element_type.80), channel_id=1, source_target_pairs={{0,16},{4,20},{8,24},{12,28},{16,32},{20,36},{24,40},{28,44},{32,4... | collective-permute-start | bytes 98312 | tf_op jit(solution)/shard_map/ppermute | solution.py:11
  68.8 9.4 %collective-permute-start.5 = (bf16[16,1024]{1,0:T(8,128)(2,1)S(1)}, bf16[16,1024]{1,0:T(8,128)(2,1)S(1)}, u32[]{:S(2)}, u32[]{:S(2)}) collective-permute-start(bf16[16,1024]{1,0:T(8,128)(2,1)S(1)} %fusion.29), channel_id=1, source_target_pairs={{0,16},{4,20},{8,24},{12,28},{16,32},{20,36},{24,40},{28,44},{32,4... | collective-permute-start | bytes 98312 | tf_op jit(solution)/shard_map/ppermute | solution.py:11
  70.7 10.7 %collective-permute-start.6 = (bf16[16,1024]{1,0:T(8,128)(2,1)S(1)}, bf16[16,1024]{1,0:T(8,128)(2,1)S(1)}, u32[]{:S(2)}, u32[]{:S(2)}) collective-permute-start(bf16[16,1024]{1,0:T(8,128)(2,1)S(1)} %fusion.29), channel_id=1, source_target_pairs={{0,32},{4,36},{8,40},{12,44},{16,48},{20,52},{24,56},{28,60},{32,6... | collective-permute-start | bytes 98312 | tf_op jit(solution)/shard_map/ppermute | solution.py:11
  73.1 11.6 %collective-permute-start.7 = (bf16[16,1024]{1,0:T(8,128)(2,1)S(1)}, bf16[16,1024]{1,0:T(8,128)(2,1)S(1)}, u32[]{:S(2)}, u32[]{:S(2)}) collective-permute-start(bf16[16,1024]{1,0:T(8,128)(2,1)S(1)} %fusion.29), channel_id=1, source_target_pairs={{0,48},{4,52},{8,56},{12,60},{16,64},{20,68},{24,72},{28,76},{32,8... | collective-permute-start | bytes 98312 | tf_op jit(solution)/shard_map/ppermute | solution.py:11
  84.8 5.0 %collective-permute-start.10 = (bf16[16,1024]{1,0:T(8,128)(2,1)S(1)}, bf16[16,1024]{1,0:T(8,128)(2,1)S(1)}, u32[]{:S(2)}, u32[]{:S(2)}) collective-permute-start(bf16[16,1024]{1,0:T(8,128)(2,1)S(1)} %get-tuple-element.2), channel_id=1, source_target_pairs={{0,192},{4,196},{8,200},{12,204},{16,208},{20,212},{24,216},{28,22... | collective-permute-start | bytes 98312 | tf_op jit(solution)/shard_map/ppermute | solution.py:11
  85.5 12.1 %collective-permute-start.8 = (bf16[16,1024]{1,0:T(8,128)(2,1)S(1)}, bf16[16,1024]{1,0:T(8,128)(2,1)S(1)}, u32[]{:S(2)}, u32[]{:S(2)}) collective-permute-start(bf16[16,1024]{1,0:T(8,128)(2,1)S(1)} %get-tuple-element.2), channel_id=1, source_target_pairs={{0,64},{4,68},{8,72},{12,76},{16,80},{20,84},{24,88},{28,92},{32,9... | collective-permute-start | bytes 98312 | tf_op jit(solution)/shard_map/ppermute | solution.py:11
  87.4 10.2 %collective-permute-start.9 = (bf16[16,1024]{1,0:T(8,128)(2,1)S(1)}, bf16[16,1024]{1,0:T(8,128)(2,1)S(1)}, u32[]{:S(2)}, u32[]{:S(2)}) collective-permute-start(bf16[16,1024]{1,0:T(8,128)(2,1)S(1)} %get-tuple-element.2), channel_id=1, source_target_pairs={{0,128},{4,132},{8,136},{12,140},{16,144},{20,148},{24,152},{28,15... | collective-permute-start | bytes 98312 | tf_op jit(solution)/shard_map/ppermute | solution.py:11
  88.7 8.9 %copy-start.8 = (f32[16,1024]{1,0:T(8,128)S(1)}, f32[16,1024]{1,0:T(8,128)}, u32[]{:S(2)}) copy-start(f32[16,1024]{1,0:T(8,128)} %param.19) | copy-start | bytes 196612

commit v5 on v3

--- a/solution.py
+++ b/solution.py
@@ -144,10 +144,9 @@
     u_rows = filt - 1 + short_rim
     pack = 16
     sent_rows = -(-u_rows // pack) * pack
-    tail = slice(tokens - sent_rows - short_rim, tokens)
-    sk_tail = short_conv(k_mr[tail], short_taps[1], sent_rows)
-    sv_tail = short_conv(v_mr[tail], short_taps[2], sent_rows)
-    u_tail = (sk_tail * sv_tail).astype(jnp.bfloat16)
+    inner = tokens - short_rim
+    u_loc = (short_conv(k_mr, short_taps[1], inner) * short_conv(v_mr, short_taps[2], inner)).astype(jnp.bfloat16)
+    u_tail = u_loc[inner - sent_rows :]
     q_rows = 2 * short_rim
     rims = [
         q_mr[tokens - q_rows :],
@@ -171,12 +170,14 @@
     at += short_rim
     kl_rim = got[at : at + short_rim]
 
-    sk = short_conv(jnp.concatenate([k_rim, k_mr]), short_taps[1], tokens)
-    sv = short_conv(jnp.concatenate([v_rim, v_mr]), short_taps[2], tokens)
-    u_mr = (sk * sv).astype(jnp.bfloat16)
-    u_ext = jnp.concatenate([u_rim, u_mr]).astype(jnp.float32)
+    sk = short_conv(jnp.concatenate([k_rim, k_mr[:short_rim]]), short_taps[1], short_rim)
+    sv = short_conv(jnp.concatenate([v_rim, v_mr[:short_rim]]), short_taps[2], short_rim)
+    u_head = (sk * sv).astype(jnp.bfloat16)
     ext_rows = tokens + short_rim
-    mr_long = long_conv(u_ext, mr_taps)
+    local_rows = inner - (filt - 1)
+    head = ext_rows - local_rows
+    u_ext = jnp.concatenate([u_rim, u_head, u_loc[: head + filt - 1 - u_rows - short_rim]]).astype(jnp.float32)
+    mr_long = jnp.concatenate([long_conv(u_ext, mr_taps), long_conv(u_loc.astype(jnp.float32), mr_taps)])
     sq = short_conv(jnp.concatenate([q_rim, q_mr]), short_taps[0], ext_rows)
     mixer_ext = to_bf16(sq * mr_long)
     mixer_mr = mixer_ext[short_rim:].astype(jnp.bfloat16)

time: 108 us -> 105 us (0.972)
  waiting for transfers between devices: 37.1 us -> 33.4 us
    ppermute x11, waiting for transfers between devices: 37.1 us -> 33.4 us  [shifted(): return lax.ppermute(shard, axis, pairs)]
    concatenate x1, local copies, waits for them, and re-layouts: 0.18 us -> 2.61 us  [shards(): jnp.concatenate([u_tail, jnp.concatenate(rims + [fill])])]
    rev x1, local copies, waits for them, and re-layouts: 2.62 us -> 0.24 us  [long_conv(): kernel = taps[::-1][:, None, :]]
    unnamed x22 -> x20, local copies, waits for them, and re-layouts: 0.06 us -> 1.29 us
    conv_general_dilated x1 -> x2, matrix products: 11 us -> 11.8 us  [long_conv(): lax.conv_general_dilated(extended[None], kernel, (1,), 'VALID', dimension...]
  transfers between devices with their start and end apart: 11 -> 11, of which waited for: 9 -> 10; matrix products, arithmetic and copies ran while one was open for 4% -> 7% of each run, Pallas kernels for 0% -> 0%
where the time goes in v5:
time: 105 us; the launch traced here: 104 us
  waiting for transfers between devices  33.4 us (32%)
  starting transfers between devices  24 us (23%)
  matrix products  11.8 us (11%)
  Pallas kernels  9.91 us (9%)
  other arithmetic  9.88 us (9%)
  local copies, waits for them, and re-layouts  8.67 us (8%)
  blocking collectives  5.77 us (5%)
    ppermute x11, waiting for transfers between devices, shifted(): return lax.ppermute(shard, axis, pairs)  33.4 us
    ppermute x11, starting transfers between devices, shifted(): return lax.ppermute(shard, axis, pairs)  24 us
    conv_general_dilated x2, matrix products, long_conv(): lax.conv_general_dilated(extended[None], kernel, (1,), 'VALID', dimension...  11.8 us
    pallas_call x1, Pallas kernels, recur_output(): pl.pallas_call(_output_kernel, out_shape=jax.ShapeDtypeStruct(u.shape, jn...  6.78 us
    psum x1, blocking collectives, shards(): totals = lax.psum(jnp.sum(mixer_ext * mixer_ext, axis=1), 'mp')  5.77 us
    pallas_call x1, Pallas kernels, recur_ends(): pl.pallas_call(_ends_kernel, out_shape=jax.ShapeDtypeStruct(a.shape, jnp....  3.13 us
    concatenate x1, local copies, waits for them, and re-layouts, shards(): jnp.concatenate([u_tail, jnp.concatenate(rims + [fill])])  2.61 us
    convert_element_type x1, other arithmetic, shards(): mixer_li = (lq * long_li).astype(jnp.bfloat16)  2.41 us
  transfers between devices with their start and end apart: 11, of which 10 were waited for; matrix products, arithmetic and copies ran while one was open for 7% of the time, Pallas kernels for 0%

profile of v5, /device:TPU:6, one launch (start us, length us, event | category | flops | bytes accessed | tf_op | source)
XLA Modules:
  0.0 104.4 jit_solution(18151148424331575628)
XLA Ops:
  0.6 1.2 %convert_element_type.72 = f32[256,1024]{1,0:T(8,128)S(1)} convert(bf16[256,1024]{1,0:T(8,128)(2,1)} %param.11) | non-fusion elementwise | flops 262144 | bytes 1572864 | tf_op jit(solution)/shard_map/convert_element_type | solution.py:20
  1.9 0.9 fusion.35
  3.0 0.1 copy-done.3
  3.1 0.1 copy-done.2
  3.4 0.7 fusion.18
  4.1 2.6 %concatenate.24 = bf16[160,1024]{1,0:T(8,128)(2,1)} concatenate(bf16[144,1024]{1,0:T(8,128)(2,1)S(1)} %slice.289, bf16[4,1024]{1,0:T(4,128)(2,1)S(1)} %slice.239, bf16[2,1024]{1,0:T(2,128)(2,1)S(1)} %get-tuple-element.7, bf16[2,1024]{1,0:T(2,128)(2,1)S(1)} %get-tuple-element.35, bf16[2,1024]{1,0:T(2,128)(2,1)S(1)} %slice.242, bf16[2,1024]{1,0:T(2,128)(2,1)S(1)} %slice.243, ...), dimensions={0} | concatenate | bytes 655360 | tf_op jit(solution)/shard_map/concatenate | solution.py:160
  6.7 3.5 %collective-permute-start = (bf16[160,1024]{1,0:T(8,128)(2,1)}, bf16[160,1024]{1,0:T(8,128)(2,1)}, u32[]{:S(2)}, u32[]{:S(2)}) collective-permute-start(bf16[160,1024]{1,0:T(8,128)(2,1)} %concatenate.24), channel_id=1, source_target_pairs={{0,4},{4,8},{8,12},{12,16},{16,20},{20,24},{24,28},{28,32},{32,36}... | collective-permute-start | bytes 983048 | tf_op jit(solution)/shard_map/ppermute | solution.py:11
  10.2 0.2 rev.4
  10.5 5.8 %fusion.22 = f32[1,127,1024]{2,0,1:T(1,128)S(1)} fusion(bf16[1,254,1024]{2,1,0:T(8,128)(2,1)S(1)} %bitcast.28, f32[128,1,1024]{2,0,1:T(8,128)S(1)} %bitcast.31), kind=kOutput, calls=%fused_computation.43 | convolution fusion | flops 199753728 | bytes 1564672 | tf_op jit(solution)/shard_map/conv_general_dilated | solution.py:30
  16.4 0.7 copy-done
  17.1 0.6 negate_exponential_fusion.a_ref
  17.7 8.1 %collective-permute-done = bf16[160,1024]{1,0:T(8,128)(2,1)} collective-permute-done((bf16[160,1024]{1,0:T(8,128)(2,1)}, bf16[160,1024]{1,0:T(8,128)(2,1)}, u32[]{:S(2)}, u32[]{:S(2)}) %collective-permute-start) | collective-permute-done | bytes 327712 | tf_op jit(solution)/shard_map/ppermute | solution.py:11
  25.8 0.8 fusion.37
  26.7 1.0 slice.294
  27.8 6.0 %fusion.4 = f32[1,131,1024]{2,0,1:T(1,128)S(1)} fusion(bf16[1,258,1024]{2,1,0:T(8,128)(2,1)S(1)} %maximum_bitcast_fusion, f32[128,1,1024]{2,0,1:T(8,128)S(1)} %bitcast.32), kind=kOutput, calls=%fused_computation.9 | convolution fusion | flops 206045184 | bytes 1589248 | tf_op jit(solution)/shard_map/conv_general_dilated | solution.py:30
  34.0 0.7 slice.290
  34.7 0.1 maximum_convert_fusion
  34.9 0.7 multiply_reduce_fusion
  35.5 5.8 %psum.7 = f32[258]{0:T(512)S(1)} all-reduce(f32[258]{0:T(512)S(1)} %get-tuple-element.4), channel_id=1, replica_groups=mesh['ctx'=64,'mp'=4] {'mp'}, use_global_device_ids=true, to_apply=%region_1.0 | all-reduce | flops 258 | bytes 2064 | tf_op jit(solution)/shard_map/psum | solution.py:185
  41.3 0.1 maximum_convert_fusion.2
  41.5 0.2 multiply_reduce-precision_fusion
  41.7 1.7 %fusion.8.u_ref = f32[256,1024]{1,0:T(8,128)} fusion(f32[258,1024]{1,0:T(8,128)S(1)} %multiply_reduce-precision_fusion, f32[258,1024]{1,0:T(8,128)S(1)} %maximum_convert_fusion.2, f32[1024]{0:T(1024)S(1)} %bitcast.49, f32[1024]{0:T(1024)S(1)} %bitcast.50, f32[1024]{0:T(1024)S(1)} %bitcast.45, f32[1024]{0:T(1024)S(1)} %bitcast.46, f32[1024]{0:T(1024)S(1)} %bitcast.47, ...), kind=kLoop, calls=%fused_computation.14 | loop fusion | flops 3145728 | bytes 7364608 | tf_op jit(solution)/shard_map/reduce_precision | solution.py:15
  43.4 3.1 %shard_map.113 = f32[16,1024]{1,0:T(8,128)} custom-call(f32[256,1024]{1,0:T(8,128)} %fusion.8.u_ref, f32[16,1024]{1,0:T(8,128)} %negate_exponential_fusion.a_ref), custom_call_target="tpu_custom_call" | custom-call | flops 8388608 | bytes 1179648 | tf_op jit(solution)/shard_map/pallas_call | solution.py:105
  46.5 0.8 convert_element_type.81
  47.3 1.9 %collective-permute-start.4 = (bf16[16,1024]{1,0:T(8,128)(2,1)S(1)}, bf16[16,1024]{1,0:T(8,128)(2,1)S(1)}, u32[]{:S(2)}, u32[]{:S(2)}) collective-permute-start(bf16[16,1024]{1,0:T(8,128)(2,1)S(1)} %convert_element_type.81), channel_id=1, source_target_pairs={{0,16},{4,20},{8,24},{12,28},{16,32},{20,36},{24,40},{28,44},{32,4... | collective-permute-start | bytes 98312 | tf_op jit(solution)/shard_map/ppermute | solution.py:11
  49.3 1.9 %collective-permute-start.3 = (bf16[16,1024]{1,0:T(8,128)(2,1)S(1)}, bf16[16,1024]{1,0:T(8,128)(2,1)S(1)}, u32[]{:S(2)}, u32[]{:S(2)}) collective-permute-start(bf16[16,1024]{1,0:T(8,128)(2,1)S(1)} %convert_element_type.81), channel_id=1, source_target_pairs={{0,12},{4,16},{8,20},{12,24},{16,28},{20,32},{24,36},{28,40},{32,4... | collective-permute-start | bytes 98312 | tf_op jit(solution)/shard_map/ppermute | solution.py:11
  51.2 1.9 %collective-permute-start.2 = (bf16[16,1024]{1,0:T(8,128)(2,1)S(1)}, bf16[16,1024]{1,0:T(8,128)(2,1)S(1)}, u32[]{:S(2)}, u32[]{:S(2)}) collective-permute-start(bf16[16,1024]{1,0:T(8,128)(2,1)S(1)} %convert_element_type.81), channel_id=1, source_target_pairs={{0,8},{4,12},{8,16},{12,20},{16,24},{20,28},{24,32},{28,36},{32,40... | collective-permute-start | bytes 98312 | tf_op jit(solution)/shard_map/ppermute | solution.py:11
  53.1 2.2 %collective-permute-start.1 = (bf16[16,1024]{1,0:T(8,128)(2,1)S(1)}, bf16[16,1024]{1,0:T(8,128)(2,1)S(1)}, u32[]{:S(2)}, u32[]{:S(2)}) collective-permute-start(bf16[16,1024]{1,0:T(8,128)(2,1)S(1)} %convert_element_type.81), channel_id=1, source_target_pairs={{0,4},{4,8},{8,12},{12,16},{16,20},{20,24},{24,28},{28,32},{32,36}... | collective-permute-start | bytes 98312 | tf_op jit(solution)/shard_map/ppermute | solution.py:11
  55.4 1.4 %collective-permute-done.4 = bf16[16,1024]{1,0:T(8,128)(2,1)S(1)} collective-permute-done((bf16[16,1024]{1,0:T(8,128)(2,1)S(1)}, bf16[16,1024]{1,0:T(8,128)(2,1)S(1)}, u32[]{:S(2)}, u32[]{:S(2)}) %collective-permute-start.4) | collective-permute-done | bytes 32800 | tf_op jit(solution)/shard_map/ppermute | solution.py:11
  56.8 2.8 %collective-permute-done.3 = bf16[16,1024]{1,0:T(8,128)(2,1)S(1)} collective-permute-done((bf16[16,1024]{1,0:T(8,128)(2,1)S(1)}, bf16[16,1024]{1,0:T(8,128)(2,1)S(1)}, u32[]{:S(2)}, u32[]{:S(2)}) %collective-permute-start.3) | collective-permute-done | bytes 32800 | tf_op jit(solution)/shard_map/ppermute | solution.py:11
  59.6 3.4 %collective-permute-done.2 = bf16[16,1024]{1,0:T(8,128)(2,1)S(1)} collective-permute-done((bf16[16,1024]{1,0:T(8,128)(2,1)S(1)}, bf16[16,1024]{1,0:T(8,128)(2,1)S(1)}, u32[]{:S(2)}, u32[]{:S(2)}) %collective-permute-start.2) | collective-permute-done | bytes 32800 | tf_op jit(solution)/shard_map/ppermute | solution.py:11
  63.0 1.6 %collective-permute-done.1 = bf16[16,1024]{1,0:T(8,128)(2,1)S(1)} collective-permute-done((bf16[16,1024]{1,0:T(8,128)(2,1)S(1)}, bf16[16,1024]{1,0:T(8,128)(2,1)S(1)}, u32[]{:S(2)}, u32[]{:S(2)}) %collective-permute-start.1) | collective-permute-done | bytes 32800 | tf_op jit(solution)/shard_map/ppermute | solution.py:11
  64.7 2.7 %collective-permute-start.7 = (bf16[16,1024]{1,0:T(8,128)(2,1)S(1)}, bf16[16,1024]{1,0:T(8,128)(2,1)S(1)}, u32[]{:S(2)}, u32[]{:S(2)}) collective-permute-start(bf16[16,1024]{1,0:T(8,128)(2,1)S(1)} %fusion.32), channel_id=1, source_target_pairs={{0,48},{4,52},{8,56},{12,60},{16,64},{20,68},{24,72},{28,76},{32,8... | collective-permute-start | bytes 98312 | tf_op jit(solution)/shard_map/ppermute | solution.py:11
  67.4 3.2 %collective-permute-start.6 = (bf16[16,1024]{1,0:T(8,128)(2,1)S(1)}, bf16[16,1024]{1,0:T(8,128)(2,1)S(1)}, u32[]{:S(2)}, u32[]{:S(2)}) collective-permute-start(bf16[16,1024]{1,0:T(8,128)(2,1)S(1)} %fusion.32), channel_id=1, source_target_pairs={{0,32},{4,36},{8,40},{12,44},{16,48},{20,52},{24,56},{28,60},{32,6... | collective-permute-start | bytes 98312 | tf_op jit(solution)/shard_map/ppermute | solution.py:11
  70.7 2.7 %collective-permute-start.5 = (bf16[16,1024]{1,0:T(8,128)(2,1)S(1)}, bf16[16,1024]{1,0:T(8,128)(2,1)S(1)}, u32[]{:S(2)}, u32[]{:S(2)}) collective-permute-start(bf16[16,1024]{1,0:T(8,128)(2,1)S(1)} %fusion.32), channel_id=1, source_target_pairs={{0,16},{4,20},{8,24},{12,28},{16,32},{20,36},{24,40},{28,44},{32,4... | collective-permute-start | bytes 98312 | tf_op jit(solution)/shard_map/ppermute | solution.py:11
  73.4 2.6 %collective-permute-done.7 = bf16[16,1024]{1,0:T(8,128)(2,1)S(1)} collective-permute-done((bf16[16,1024]{1,0:T(8,128)(2,1)S(1)}, bf16[16,1024]{1,0:T(8,128)(2,1)S(1)}, u32[]{:S(2)}, u32[]{:S(2)}) %collective-permute-start.7) | collective-permute-done | bytes 32800 | tf_op jit(solution)/shard_map/ppermute | solution.py:11
  76.0 1.8 %collective-permute-done.6 = bf16[16,1024]{1,0:T(8,128)(2,1)S(1)} collective-permute-done((bf16[16,1024]{1,0:T(8,128)(2,1)S(1)}, bf16[16,1024]{1,0:T(8,128)(2,1)S(1)}, u32[]{:S(2)}, u32[]{:S(2)}) %collective-permute-start.6) | collective-permute-done | bytes 32800 | tf_op jit(solution)/shard_map/ppermute | solution.py:11
  77.8 2.5 %collective-permute-done.5 = bf16[16,1024]{1,0:T(8,128)(2,1)S(1)} collective-permute-done((bf16[16,1024]{1,0:T(8,128)(2,1)S(1)}, bf16[16,1024]{1,0:T(8,128)(2,1)S(1)}, u32[]{:S(2)}, u32[]{:S(2)}) %collective-permute-start.5) | collective-permute-done | bytes 32800 | tf_op jit(solution)/shard_map/ppermute | solution.py:11
  80.4 0.7 collective-permute-start.10
  81.1 1.3 %collective-permute-start.9 = (bf16[16,1024]{1,0:T(8,128)(2,1)S(1)}, bf16[16,1024]{1,0:T(8,128)(2,1)S(1)}, u32[]{:S(2)}, u32[]{:S(2)}) collective-permute-start(bf16[16,1024]{1,0:T(8,128)(2,1)S(1)} %get-tuple-element.2), channel_id=1, source_target_pairs={{0,128},{4,132},{8,136},{12,140},{16,144},{20,148},{24,152},{28,15... | collective-permute-start | bytes 98312 | tf_op jit(solution)/shard_map/ppermute | solution.py:11
  82.4 1.9 %collective-permute-start.8 = (bf16[16,1024]{1,0:T(8,128)(2,1)S(1)}, bf16[16,1024]{1,0:T(8,128)(2,1)S(1)}, u32[]{:S(2)}, u32[]{:S(2)}) collective-permute-start(bf16[16,1024]{1,0:T(8,128)(2,1)S(1)} %get-tuple-element.2), channel_id=1, source_target_pairs={{0,64},{4,68},{8,72},{12,76},{16,80},{20,84},{24,88},{28,92},{32,9... | collective-permute-start | bytes 98312 | tf_op jit(solution)/shard_map/ppermute | solution.py:11
  84.3 0.1 maximum_convert_fusion.1
  84.5 0.9 slice.441
  85.4 3.0 %collective-permute-done.9 = bf16[16,1024]{1,0:T(8,128)(2,1)S(1)} collective-permute-done((bf16[16,1024]{1,0:T(8,128)(2,1)S(1)}, bf16[16,1024]{1,0:T(8,128)(2,1)S(1)}, u32[]{:S(2)}, u32[]{:S(2)}) %collective-permute-start.9) | collective-permute-done | bytes 32800 | tf_op jit(solution)/shard_map/ppermute | solution.py:11
  88.4 6.1 %collective-permute-done.8 = bf16[16,1024]{1,0:T(8,128)(2,1)S(1)} collective-permute-done((bf16[16,1024]{1,0:T(8,128)(2,1)S(1)}, bf16[16,1024]{1,0:T(8,128)(2,1)S(1)}, u32[]{:S(2)}, u32[]{:S(2)}) %collective-permute-start.8) | collective-permute-done | bytes 32800 | tf_op jit(solution)/shard_map/ppermute | solution.py:11
  94.5 0.7 multiply_add_fusion
  95.2 6.8 %shard_map.114 = f32[256,1024]{1,0:T(8,128)} custom-call(f32[256,1024]{1,0:T(8,128)} %fusion.8.u_ref, f32[16,1024]{1,0:T(8,128)} %negate_exponential_fusion.a_ref, f32[16,1024]{1,0:T(8,128)} %get-tuple-element.33.w_ref, f32[16,1024]{1,0:T(8,128)} %get-tuple-element.32.s0_ref), custom_call_target="tpu_custom_call" | custom-call | flops 16777216 | bytes 2293760 | tf_op jit(solution)/shard_map/pallas_call | solution.py:119
  102.0 2.4 %fusion.14 = bf16[256,1024]{1,0:T(8,128)(2,1)} fusion(f32[258,1024]{1,0:T(8,128)S(1)} %maximum_convert_fusion.1, f32[256,1024]{1,0:T(8,128)} %shard_map.114, f32[1024]{0:T(1024)S(1)} %bitcast.52, f32[1024]{0:T(1024)S(1)} %bitcast.53, f32[1024]{0:T(1024)S(1)} %bitcast.51), kind=kLoop, calls=%fused_computation.26 | loop fusion | flops 2097152 | bytes 4730880 | tf_op jit(solution)/shard_map/convert_element_type | solution.py:192
  (33 shorter events, 0.9 us)
Async XLA Ops:
  0.6 1.2 %copy-start.1 = (bf16[256,1024]{1,0:T(8,128)(2,1)S(1)}, bf16[256,1024]{1,0:T(8,128)(2,1)}, u32[]{:S(2)}) copy-start(bf16[256,1024]{1,0:T(8,128)(2,1)} %param.12) | copy-start | bytes 1572868
  0.6 2.6 %copy-start.7 = (f32[6,3,1024]{2,1,0:T(4,128)S(1)}, f32[6,3,1024]{2,1,0:T(4,128)}, u32[]{:S(2)}) copy-start(f32[6,3,1024]{2,1,0:T(4,128)} %param.15) | copy-start | bytes 221188
  1.9 1.1 %copy-start.4 = (bf16[256,1024]{1,0:T(8,128)(2,1)S(1)}, bf16[256,1024]{1,0:T(8,128)(2,1)}, u32[]{:S(2)}) copy-start(bf16[256,1024]{1,0:T(8,128)(2,1)} %param.13) | copy-start | bytes 1572868
  1.9 1.2 %copy-start.3 = (bf16[256,1024]{1,0:T(8,128)(2,1)S(1)}, bf16[256,1024]{1,0:T(8,128)(2,1)}, u32[]{:S(2)}) copy-start(bf16[256,1024]{1,0:T(8,128)(2,1)} %param.14) | copy-start | bytes 1572868
  1.9 1.4 %copy-start.2 = (bf16[256,1024]{1,0:T(8,128)(2,1)S(1)}, bf16[256,1024]{1,0:T(8,128)(2,1)}, u32[]{:S(2)}) copy-start(bf16[256,1024]{1,0:T(8,128)(2,1)} %param.10) | copy-start | bytes 1572868
  4.0 6.2 %copy-start.5 = (f32[128,1024]{1,0:T(8,128)S(1)}, f32[128,1024]{1,0:T(8,128)}, u32[]{:S(2)}) copy-start(f32[128,1024]{1,0:T(8,128)} %param.16) | copy-start | bytes 1572868
  6.7 19.1 %collective-permute-start = (bf16[160,1024]{1,0:T(8,128)(2,1)}, bf16[160,1024]{1,0:T(8,128)(2,1)}, u32[]{:S(2)}, u32[]{:S(2)}) collective-permute-start(bf16[160,1024]{1,0:T(8,128)(2,1)} %concatenate.24), channel_id=1, source_target_pairs={{0,4},{4,8},{8,12},{12,16},{16,20},{20,24},{24,28},{28,32},{32,36}... | collective-permute-start | bytes 983048 | tf_op jit(solution)/shard_map/ppermute | solution.py:11
  16.2 0.8 copy-start
  35.5 5.9 %copy-start.8 = (f32[1024]{0:T(1024)S(1)}, f32[1024]{0:T(1024)}, u32[]{:S(2)}) copy-start(f32[1024]{0:T(1024)} %param.17) | copy-start | bytes 12292
  47.3 9.4 %collective-permute-start.4 = (bf16[16,1024]{1,0:T(8,128)(2,1)S(1)}, bf16[16,1024]{1,0:T(8,128)(2,1)S(1)}, u32[]{:S(2)}, u32[]{:S(2)}) collective-permute-start(bf16[16,1024]{1,0:T(8,128)(2,1)S(1)} %convert_element_type.81), channel_id=1, source_target_pairs={{0,16},{4,20},{8,24},{12,28},{16,32},{20,36},{24,40},{28,44},{32,4... | collective-permute-start | bytes 98312 | tf_op jit(solution)/shard_map/ppermute | solution.py:11
  49.3 10.3 %collective-permute-start.3 = (bf16[16,1024]{1,0:T(8,128)(2,1)S(1)}, bf16[16,1024]{1,0:T(8,128)(2,1)S(1)}, u32[]{:S(2)}, u32[]{:S(2)}) collective-permute-start(bf16[16,1024]{1,0:T(8,128)(2,1)S(1)} %convert_element_type.81), channel_id=1, source_target_pairs={{0,12},{4,16},{8,20},{12,24},{16,28},{20,32},{24,36},{28,40},{32,4... | collective-permute-start | bytes 98312 | tf_op jit(solution)/shard_map/ppermute | solution.py:11
  51.2 11.8 %collective-permute-start.2 = (bf16[16,1024]{1,0:T(8,128)(2,1)S(1)}, bf16[16,1024]{1,0:T(8,128)(2,1)S(1)}, u32[]{:S(2)}, u32[]{:S(2)}) collective-permute-start(bf16[16,1024]{1,0:T(8,128)(2,1)S(1)} %convert_element_type.81), channel_id=1, source_target_pairs={{0,8},{4,12},{8,16},{12,20},{16,24},{20,28},{24,32},{28,36},{32,40... | collective-permute-start | bytes 98312 | tf_op jit(solution)/shard_map/ppermute | solution.py:11
  53.1 11.5 %collective-permute-start.1 = (bf16[16,1024]{1,0:T(8,128)(2,1)S(1)}, bf16[16,1024]{1,0:T(8,128)(2,1)S(1)}, u32[]{:S(2)}, u32[]{:S(2)}) collective-permute-start(bf16[16,1024]{1,0:T(8,128)(2,1)S(1)} %convert_element_type.81), channel_id=1, source_target_pairs={{0,4},{4,8},{8,12},{12,16},{16,20},{20,24},{24,28},{28,32},{32,36}... | collective-permute-start | bytes 98312 | tf_op jit(solution)/shard_map/ppermute | solution.py:11
  64.7 11.3 %collective-permute-start.7 = (bf16[16,1024]{1,0:T(8,128)(2,1)S(1)}, bf16[16,1024]{1,0:T(8,128)(2,1)S(1)}, u32[]{:S(2)}, u32[]{:S(2)}) collective-permute-start(bf16[16,1024]{1,0:T(8,128)(2,1)S(1)} %fusion.32), channel_id=1, source_target_pairs={{0,48},{4,52},{8,56},{12,60},{16,64},{20,68},{24,72},{28,76},{32,8... | collective-permute-start | bytes 98312 | tf_op jit(solution)/shard_map/ppermute | solution.py:11
  67.4 10.3 %collective-permute-start.6 = (bf16[16,1024]{1,0:T(8,128)(2,1)S(1)}, bf16[16,1024]{1,0:T(8,128)(2,1)S(1)}, u32[]{:S(2)}, u32[]{:S(2)}) collective-permute-start(bf16[16,1024]{1,0:T(8,128)(2,1)S(1)} %fusion.32), channel_id=1, source_target_pairs={{0,32},{4,36},{8,40},{12,44},{16,48},{20,52},{24,56},{28,60},{32,6... | collective-permute-start | bytes 98312 | tf_op jit(solution)/shard_map/ppermute | solution.py:11
  70.7 9.6 %collective-permute-start.5 = (bf16[16,1024]{1,0:T(8,128)(2,1)S(1)}, bf16[16,1024]{1,0:T(8,128)(2,1)S(1)}, u32[]{:S(2)}, u32[]{:S(2)}) collective-permute-start(bf16[16,1024]{1,0:T(8,128)(2,1)S(1)} %fusion.32), channel_id=1, source_target_pairs={{0,16},{4,20},{8,24},{12,28},{16,32},{20,36},{24,40},{28,44},{32,4... | collective-permute-start | bytes 98312 | tf_op jit(solution)/shard_map/ppermute | solution.py:11
  80.4 5.0 %collective-permute-start.10 = (bf16[16,1024]{1,0:T(8,128)(2,1)S(1)}, bf16[16,1024]{1,0:T(8,128)(2,1)S(1)}, u32[]{:S(2)}, u32[]{:S(2)}) collective-permute-start(bf16[16,1024]{1,0:T(8,128)(2,1)S(1)} %get-tuple-element.2), channel_id=1, source_target_pairs={{0,192},{4,196},{8,200},{12,204},{16,208},{20,212},{24,216},{28,22... | collective-permute-start | bytes 98312 | tf_op jit(solution)/shard_map/ppermute | solution.py:11
  81.1 7.3 %collective-permute-start.9 = (bf16[16,1024]{1,0:T(8,128)(2,1)S(1)}, bf16[16,1024]{1,0:T(8,128)(2,1)S(1)}, u32[]{:S(2)}, u32[]{:S(2)}) collective-permute-start(bf16[16,1024]{1,0:T(8,128)(2,1)S(1)} %get-tuple-element.2), channel_id=1, source_target_pairs={{0,128},{4,132},{8,136},{12,140},{16,144},{20,148},{24,152},{28,15... | collective-permute-start | bytes 98312 | tf_op jit(solution)/shard_map/ppermute | solution.py:11
  82.4 12.1 %collective-permute-start.8 = (bf16[16,1024]{1,0:T(8,128)(2,1)S(1)}, bf16[16,1024]{1,0:T(8,128)(2,1)S(1)}, u32[]{:S(2)}, u32[]{:S(2)}) collective-permute-start(bf16[16,1024]{1,0:T(8,128)(2,1)S(1)} %get-tuple-element.2), channel_id=1, source_target_pairs={{0,64},{4,68},{8,72},{12,76},{16,80},{20,84},{24,88},{28,92},{32,9... | collective-permute-start | bytes 98312 | tf_op jit(solution)/shard_map/ppermute | solution.py:11
  84.3 10.2 %copy-start.6 = (f32[16,1024]{1,0:T(8,128)S(1)}, f32[16,1024]{1,0:T(8,128)}, u32[]{:S(2)}) copy-start(f32[16,1024]{1,0:T(8,128)} %param.19) | copy-start | bytes 196612
